TPU v7x, 768 devices: a whole 4x8x12 slice. The times are simulated.
768 devices in a mesh: seq: 16 (over x, y_hi), mp: 48 (over z, y_lo, core).
Axes of the slice: x: 4, y: 8 (y_hi: 4, y_lo: 2; y = y_hi * 2 + y_lo), z: 12, core: 2. Of those that a mesh axis runs over, the one named last changes fastest.
Arguments:
- queries: bfloat16 [16, 48, 1280, 256], P('seq', 'mp'), may hold values from -6 to 6
- key_rows: bfloat16 [16, 48, 1280, 128], P('seq', 'mp'), may hold values from -6 to 6
- value_rows: bfloat16 [16, 48, 1280, 128], P('seq', 'mp'), may hold values from -6 to 6
Outputs:
- attended: bfloat16 [16, 48, 1280, 256], P('seq', 'mp')
All inputs are finite; a program needn't handle non-finite values.
Results may differ from a plain program's by a relative error of at most 0.0055.
Values may be sent and summed in bfloat16 or wider, within the bound.
No kernel may reach another device: no remote copies, remote signals or barrier semaphores. Data moves between devices by JAX's collectives and lax.ppermute only.
A program may use at most 64 MiB of HBM per device.

v0:
```python
import jax
import jax.numpy as jnp
from jax import lax
from jax.sharding import PartitionSpec as P

KVH = 8
QPK = 2
WINDOW = 1024


scale_factor = 168.0 ** (-0.5)


def passed_along(block, axis, distance):
    devices = range(lax.axis_size(axis))
    route = [(i - distance, i) for i in devices if i - distance in devices]
    return lax.ppermute(block, axis, route)


def block_size(total_rows):
    size_now = total_rows
    while size_now > 1024 and size_now % 2 == 0:
        size_now = size_now // 2
    return size_now


def masked_scores(query_tile, key_tile, valid):
    raw = (
        jnp.einsum("qd,kd->qk", query_tile, key_tile, preferred_element_type=jnp.float32)
        * scale_factor
    )
    return jnp.where(valid, raw, -jnp.inf)


def joined_context(scores, value_tile):
    row_top = jnp.max(scores, axis=1, keepdims=True)
    probable = jnp.exp(scores - row_top)
    row_total = jnp.sum(probable, axis=1, keepdims=True)
    weights = probable.astype(jnp.bfloat16)
    return jnp.dot(weights, value_tile, preferred_element_type=jnp.float32) / row_total


def per_device(queries, key_rows, value_rows):
    row_count = queries.shape[2]
    head_size = key_rows.shape[3]
    model_count = lax.axis_size("mp")
    row_block = lax.axis_index("mp") // KVH
    opening = jnp.logical_and(lax.axis_index("seq") == 0, row_block == 0)
    query_local = queries[0, 0]
    local_pair = jnp.stack([key_rows[0, 0], value_rows[0, 0]])
    inside = passed_along(local_pair, "mp", KVH)
    turned = passed_along(local_pair, "mp", KVH - model_count)
    crossed = passed_along(turned, "seq", 1)
    borrowed = jnp.where(row_block == 0, crossed, inside)
    borrowed_rows = borrowed.shape[1]
    query_block = block_size(row_count)
    head_outputs = []
    for sub_head in range(QPK):
        query_head = query_local[:, sub_head * head_size : (sub_head + 1) * head_size]
        column_tiles = []
        for first_row in range(0, row_count, query_block):
            query_tile = query_head[first_row : first_row + query_block]
            low_key = max(0, first_row - WINDOW + 1)
            high_key = first_row + query_block
            halo_need = max(0, WINDOW - 1 - first_row)
            query_pos = first_row + lax.broadcasted_iota(jnp.int32, (query_block, 1), 0)
            local_pos = low_key + lax.broadcasted_iota(jnp.int32, (1, high_key - low_key), 1)
            local_valid = (local_pos <= query_pos) & (query_pos - local_pos < WINDOW)
            local_keys = local_pair[0, low_key:high_key]
            local_values = local_pair[1, low_key:high_key]
            local_scores = masked_scores(query_tile, local_keys, local_valid)
            halo_pos = lax.broadcasted_iota(jnp.int32, (1, halo_need), 1) - halo_need
            halo_valid = (query_pos - halo_pos < WINDOW) & jnp.logical_not(opening)
            halo_keys = borrowed[0, borrowed_rows - halo_need :]
            halo_values = borrowed[1, borrowed_rows - halo_need :]
            halo_scores = masked_scores(query_tile, halo_keys, halo_valid)
            all_scores = jnp.concatenate([halo_scores, local_scores], axis=1)
            all_values = jnp.concatenate([halo_values, local_values], axis=0)
            context = joined_context(all_scores, all_values)
            column_tiles.append(context.astype(jnp.bfloat16))
        head_outputs.append(jnp.concatenate(column_tiles, axis=0))
    attended = jnp.concatenate(head_outputs, axis=1)
    return attended.reshape(1, 1, row_count, QPK * head_size)


def solution(mesh):
    in_specs = (P("seq", "mp", None, None), P("seq", "mp", None, None), P("seq", "mp", None, None))
    out_specs = P("seq", "mp", None, None)
    return jax.shard_map(
        per_device, mesh=mesh, in_specs=in_specs, out_specs=out_specs, check_vma=False
    )
```

profile of v0, /device:TPU:79, one launch (start us, length us, event | category | flops | bytes accessed | tf_op | source)
XLA Modules:
  0.0 106.9 jit_solution(116588699023974619)
XLA Ops:
  0.0 1.2 %pad_maximum_fusion = bf16[2,1280,128]{2,1,0:T(8,128)(2,1)S(1)} fusion(bf16[1,1280,128]{2,1,0:T(8,128)(2,1)} %bitcast.57, bf16[1,1280,128]{2,1,0:T(8,128)(2,1)} %bitcast.61), kind=kLoop, calls=%fused_computation.54 | loop fusion | flops 327680 | bytes 1310720 | tf_op jit(solution)/shard_map/stack | solution.py:50
  1.2 1.3 %collective-permute-start = (bf16[2,1280,128]{2,1,0:T(8,128)(2,1)S(1)}, bf16[2,1280,128]{2,1,0:T(8,128)(2,1)}, u32[]{:S(2)}, u32[]{:S(2)}) collective-permute-start(bf16[2,1280,128]{2,1,0:T(8,128)(2,1)S(1)} %pad_maximum_fusion), channel_id=1, source_target_pairs={{40,0},{41,1},{42,2},{43,3},{44,4},{45,5},{46,6},{47,7},{88,48},{8... | collective-permute-start | bytes 1966088 | tf_op jit(solution)/shard_map/ppermute | solution.py:17
  2.5 6.0 %collective-permute-start.2 = (bf16[2,1280,128]{2,1,0:T(8,128)(2,1)S(1)}, bf16[2,1280,128]{2,1,0:T(8,128)(2,1)S(1)}, u32[]{:S(2)}, u32[]{:S(2)}) collective-permute-start(bf16[2,1280,128]{2,1,0:T(8,128)(2,1)S(1)} %pad_maximum_fusion), channel_id=1, source_target_pairs={{0,8},{1,9},{2,10},{3,11},{4,12},{5,13},{6,14},{7,15},{8,16},{9,17... | collective-permute-start | bytes 1966088 | tf_op jit(solution)/shard_map/ppermute | solution.py:17
  9.1 0.9 slice_bitcast_fusion.4
  10.1 2.7 %fusion.81 = (f32[640]{0:T(1024)S(1)}, f32[640,640]{0,1:T(8,128)}) fusion(bf16[1,1280,128]{2,1,0:T(8,128)(2,1)} %bitcast.62, bf16[1280,256]{1,0:T(8,128)(2,1)} %bitcast.64), kind=kOutput, calls=%fused_computation.93 | convolution fusion | flops 107724160 | bytes 1968640 | tf_op jit(solution)/shard_map/qd,kd->qk/dot_general | solution.py:29
  12.8 1.3 %fusion.77 = (f32[640]{0:T(1024)S(1)}, f32[640,640]{0,1:T(8,128)S(1)}) fusion(bf16[1,1280,128]{2,1,0:T(8,128)(2,1)S(1)} %bitcast.63, bf16[1280,256]{1,0:T(8,128)(2,1)} %bitcast.65), kind=kOutput, calls=%fused_computation.89 | convolution fusion | flops 107724160 | bytes 1968640 | tf_op jit(solution)/shard_map/qd,kd->qk/dot_general | solution.py:29
  14.1 29.2 %collective-permute-done = bf16[2,1280,128]{2,1,0:T(8,128)(2,1)} collective-permute-done((bf16[2,1280,128]{2,1,0:T(8,128)(2,1)S(1)}, bf16[2,1280,128]{2,1,0:T(8,128)(2,1)}, u32[]{:S(2)}, u32[]{:S(2)}) %collective-permute-start) | collective-permute-done | bytes 655392 | tf_op jit(solution)/shard_map/ppermute | solution.py:17
  43.3 4.2 %collective-permute-start.1 = (bf16[2,1280,128]{2,1,0:T(8,128)(2,1)}, bf16[2,1280,128]{2,1,0:T(8,128)(2,1)}, u32[]{:S(2)}, u32[]{:S(2)}) collective-permute-start(bf16[2,1280,128]{2,1,0:T(8,128)(2,1)} %collective-permute-done), channel_id=1, source_target_pairs={{0,48},{48,96},{96,144},{144,192},{192,240},{240,288},{288,336},{3... | collective-permute-start | bytes 1966088 | tf_op jit(solution)/shard_map/ppermute | solution.py:17
  48.1 3.8 %fusion.79 = (f32[640]{0:T(1024)S(1)}, f32[640,1280]{1,0:T(8,128)}) fusion(bf16[1,1,1280,128]{3,2,1,0:T(8,128)(2,1)S(1)} %copy-done.6, bf16[1280,256]{1,0:T(8,128)(2,1)} %bitcast.66, s32[640]{0:T(1024)S(1)} %iota_add_fusion), kind=kOutput, calls=%fused_computation.91 | convolution fusion | flops 215448960 | bytes 3773440 | tf_op jit(solution)/shard_map/qd,kd->qk/dot_general | solution.py:29
  51.9 2.8 %fusion.75 = (f32[640]{0:T(1024)S(1)}, f32[640,1280]{1,0:T(8,128)}) fusion(bf16[1,1,1280,128]{3,2,1,0:T(8,128)(2,1)S(1)} %copy-done.6, bf16[1280,256]{1,0:T(8,128)(2,1)S(1)} %bitcast.67, s32[640]{0:T(1024)S(1)} %iota_add_fusion), kind=kOutput, calls=%fused_computation.87 | convolution fusion | flops 215448960 | bytes 3774976 | tf_op jit(solution)/shard_map/qd,kd->qk/dot_general | solution.py:29
  54.8 24.3 %collective-permute-done.1 = bf16[2,1280,128]{2,1,0:T(8,128)(2,1)} collective-permute-done((bf16[2,1280,128]{2,1,0:T(8,128)(2,1)}, bf16[2,1280,128]{2,1,0:T(8,128)(2,1)}, u32[]{:S(2)}, u32[]{:S(2)}) %collective-permute-start.1) | collective-permute-done | bytes 655392 | tf_op jit(solution)/shard_map/ppermute | solution.py:17
  79.1 1.2 %broadcast_select_fusion = bf16[2,1280,128]{2,1,0:T(8,128)(2,1)S(1)} fusion(bf16[2,1280,128]{2,1,0:T(8,128)(2,1)} %collective-permute-done.1, bf16[2,1280,128]{2,1,0:T(8,128)(2,1)S(1)} %collective-permute-done.2, pred[]{:T(512)S(6)} %eq.8), kind=kLoop, calls=%fused_computation.56 | loop fusion | flops 327680 | bytes 1966081 | tf_op jit(solution)/shard_map/jit(_where)/select_n | solution.py:54
  80.4 2.4 %fusion.80 = (f32[640]{0:T(1024)S(1)}, f32[640,1023]{0,1:T(8,128)}) fusion(bf16[1280,256]{1,0:T(8,128)(2,1)S(1)} %bitcast.68, bf16[2,1280,128]{2,1,0:T(8,128)(2,1)S(1)} %broadcast_select_fusion, pred[]{:T(512)S(6)} %not.2, s32[1023]{0:T(1024)S(1)} %copy-done.9), kind=kOutput, calls=%fused_computation.92 | convolution fusion | flops 171536000 | bytes 3051521 | tf_op jit(solution)/shard_map/qd,kd->qk/dot_general | solution.py:29
  82.8 2.5 %fusion.76 = (f32[640]{0:T(1024)S(1)}, f32[640,1023]{0,1:T(8,128)}) fusion(bf16[1280,256]{1,0:T(8,128)(2,1)S(1)} %bitcast.69, bf16[2,1280,128]{2,1,0:T(8,128)(2,1)S(1)} %broadcast_select_fusion, pred[]{:T(512)S(6)} %not.2, s32[1023]{0:T(1024)S(1)} %copy-done.9), kind=kOutput, calls=%fused_computation.88 | convolution fusion | flops 171536000 | bytes 3051521 | tf_op jit(solution)/shard_map/qd,kd->qk/dot_general | solution.py:29
  85.3 1.3 %fusion.78 = (f32[640]{0:T(1024)S(1)}, f32[640,383]{0,1:T(8,128)}) fusion(bf16[1280,256]{1,0:T(8,128)(2,1)S(1)} %bitcast.70, bf16[2,1280,128]{2,1,0:T(8,128)(2,1)S(1)} %broadcast_select_fusion, pred[]{:T(512)S(6)} %not.2, s32[383]{0:T(512)S(1)} %copy-done.10, s32[640]{0:T(1024)S(1)} %copy-done.8), kind=kOutput, calls=%fused_computation.90 | convolution fusion | flops 64220800 | bytes 1251329 | tf_op jit(solution)/shard_map/qd,kd->qk/dot_general | solution.py:29
  86.7 1.3 %fusion.74 = (f32[640]{0:T(1024)S(1)}, f32[640,383]{0,1:T(8,128)}) fusion(bf16[1280,256]{1,0:T(8,128)(2,1)S(1)} %bitcast.71, bf16[2,1280,128]{2,1,0:T(8,128)(2,1)S(1)} %broadcast_select_fusion, pred[]{:T(512)S(6)} %not.2, s32[383]{0:T(512)S(1)} %copy-done.10, s32[640]{0:T(1024)S(1)} %copy-done.8), kind=kOutput, calls=%fused_computation.86 | convolution fusion | flops 64220800 | bytes 1251329 | tf_op jit(solution)/shard_map/qd,kd->qk/dot_general | solution.py:29
  88.0 1.5 %copy.4 = f32[640,383]{1,0:T(8,128)S(1)} copy(f32[640,383]{0,1:T(8,128)} %get-tuple-element.14) | data formatting | bytes 1960960 | tf_op jit(solution)/shard_map/jit(_where)/select_n | solution.py:32
  89.6 3.1 %fusion.14 = f32[640]{0:T(1024)S(1)} fusion(f32[640,640]{0,1:T(8,128)} %get-tuple-element.20, f32[640,1023]{0,1:T(8,128)} %get-tuple-element.18, f32[640]{0:T(1024)S(1)} %reduce_max.82), kind=kLoop, calls=%fused_computation.22 | loop fusion | flops 3192320 | bytes 4262400 | tf_op jit(solution)/shard_map/reduce_sum | solution.py:38
  96.4 1.6 %copy.5 = f32[640,383]{1,0:T(8,128)S(1)} copy(f32[640,383]{0,1:T(8,128)} %get-tuple-element.6) | data formatting | bytes 1960960 | tf_op jit(solution)/shard_map/jit(_where)/select_n | solution.py:32
  98.0 3.4 %fusion.12 = f32[640]{0:T(1024)S(1)} fusion(f32[640,1280]{1,0:T(8,128)} %get-tuple-element.16, f32[640,383]{1,0:T(8,128)S(1)} %copy.4, f32[640]{0:T(1024)S(1)} %reduce_max.85), kind=kLoop, calls=%fused_computation.20 | loop fusion | flops 3192320 | bytes 4262400 | tf_op jit(solution)/shard_map/reduce_sum | solution.py:38
  101.4 1.3 %fusion.40 = bf16[640,128]{1,0:T(8,128)(2,1)S(1)} fusion(f32[640,1280]{1,0:T(8,128)S(1)} %copy-done.1, f32[640,383]{1,0:T(8,128)S(1)} %copy.4, f32[640]{0:T(1024)S(1)} %reduce_max.85, bf16[1280,128]{1,0:T(8,128)(2,1)S(1)} %bitcast.59, bf16[383,128]{1,0:T(8,128)(2,1)S(1)} %slice_bitcast_fusion.8, f32[640]{0:T(1024)S(1)} %fusion.12), kind=kOutput, calls=%fused_computation.47 | convolution fusion | flops 276674176 | bytes 4851968 | tf_op jit(solution)/shard_map/dot_general | solution.py:40
  103.3 1.4 %fusion.8 = f32[640]{0:T(1024)S(1)} fusion(f32[640,1280]{1,0:T(8,128)S(1)} %copy-done, f32[640,383]{1,0:T(8,128)S(1)} %copy.5, f32[640]{0:T(1024)S(1)} %reduce_max.91), kind=kLoop, calls=%fused_computation.16 | loop fusion | flops 3192320 | bytes 4262400 | tf_op jit(solution)/shard_map/reduce_sum | solution.py:38
  104.7 1.3 %fusion.34 = bf16[640,128]{1,0:T(8,128)(2,1)S(1)} fusion(f32[640,1280]{1,0:T(8,128)S(1)} %copy-done, f32[640,383]{1,0:T(8,128)S(1)} %copy.5, f32[640]{0:T(1024)S(1)} %reduce_max.91, bf16[1280,128]{1,0:T(8,128)(2,1)S(1)} %bitcast.60, bf16[383,128]{1,0:T(8,128)(2,1)S(1)} %slice_bitcast_fusion.8, f32[640]{0:T(1024)S(1)} %fusion.8), kind=kOutput, calls=%fused_computation.45 | convolution fusion | flops 276674176 | bytes 4851968 | tf_op jit(solution)/shard_map/dot_general | solution.py:40
  106.0 0.9 maximum_bitcast_fusion
  (37 shorter events, 5.6 us)
Async XLA Ops:
  0.0 12.8 %copy-start.6 = (bf16[1,1,1280,128]{3,2,1,0:T(8,128)(2,1)S(1)}, bf16[1,1,1280,128]{3,2,1,0:T(8,128)(2,1)}, u32[]{:S(2)}) copy-start(bf16[1,1,1280,128]{3,2,1,0:T(8,128)(2,1)} %param.4) | copy-start | bytes 983044
  1.2 42.1 %collective-permute-start = (bf16[2,1280,128]{2,1,0:T(8,128)(2,1)S(1)}, bf16[2,1280,128]{2,1,0:T(8,128)(2,1)}, u32[]{:S(2)}, u32[]{:S(2)}) collective-permute-start(bf16[2,1280,128]{2,1,0:T(8,128)(2,1)S(1)} %pad_maximum_fusion), channel_id=1, source_target_pairs={{40,0},{41,1},{42,2},{43,3},{44,4},{45,5},{46,6},{47,7},{88,48},{8... | collective-permute-start | bytes 1966088 | tf_op jit(solution)/shard_map/ppermute | solution.py:17
  2.5 52.3 %collective-permute-start.2 = (bf16[2,1280,128]{2,1,0:T(8,128)(2,1)S(1)}, bf16[2,1280,128]{2,1,0:T(8,128)(2,1)S(1)}, u32[]{:S(2)}, u32[]{:S(2)}) collective-permute-start(bf16[2,1280,128]{2,1,0:T(8,128)(2,1)S(1)} %pad_maximum_fusion), channel_id=1, source_target_pairs={{0,8},{1,9},{2,10},{3,11},{4,12},{5,13},{6,14},{7,15},{8,16},{9,17... | collective-permute-start | bytes 1966088 | tf_op jit(solution)/shard_map/ppermute | solution.py:17
  10.1 41.8 %copy-start.7 = (s32[640]{0:T(1024)}, s32[640]{0:T(1024)S(1)}, u32[]{:S(2)}) copy-start(s32[640]{0:T(1024)S(1)} %iota_add_fusion) | copy-start | bytes 7684
  43.3 35.8 %collective-permute-start.1 = (bf16[2,1280,128]{2,1,0:T(8,128)(2,1)}, bf16[2,1280,128]{2,1,0:T(8,128)(2,1)}, u32[]{:S(2)}, u32[]{:S(2)}) collective-permute-start(bf16[2,1280,128]{2,1,0:T(8,128)(2,1)} %collective-permute-done), channel_id=1, source_target_pairs={{0,48},{48,96},{96,144},{144,192},{192,240},{240,288},{288,336},{3... | collective-permute-start | bytes 1966088 | tf_op jit(solution)/shard_map/ppermute | solution.py:17
  48.1 3.8 %copy-start.11 = (bf16[1,1,1280,256]{3,2,1,0:T(8,128)(2,1)S(1)}, bf16[1,1,1280,256]{3,2,1,0:T(8,128)(2,1)}, u32[]{:S(2)}) copy-start(bf16[1,1,1280,256]{3,2,1,0:T(8,128)(2,1)} %param.3) | copy-start | bytes 1966084
  51.9 28.4 %copy-start.9 = (s32[1023]{0:T(1024)S(1)}, s32[1023]{0:T(1024)}, u32[]{:S(2)}) copy-start(s32[1023]{0:T(1024)} %iota_add_fusion.1) | copy-start | bytes 12280
  82.8 2.5 %copy-start.8 = (s32[640]{0:T(1024)S(1)}, s32[640]{0:T(1024)}, u32[]{:S(2)}) copy-start(s32[640]{0:T(1024)} %copy-done.7) | copy-start | bytes 7684
  82.8 2.5 %copy-start.10 = (s32[383]{0:T(512)S(1)}, s32[383]{0:T(512)}, u32[]{:S(2)}) copy-start(s32[383]{0:T(512)} %iota_add_fusion.2) | copy-start | bytes 4600
  89.5 3.2 %copy-start.3 = (f32[640,1023]{0,1:T(8,128)S(1)}, f32[640,1023]{0,1:T(8,128)}, u32[]{:S(2)}) copy-start(f32[640,1023]{0,1:T(8,128)} %get-tuple-element.18) | copy-start | bytes 7856644
  89.5 3.5 %copy-start.4 = (f32[640,640]{0,1:T(8,128)S(1)}, f32[640,640]{0,1:T(8,128)}, u32[]{:S(2)}) copy-start(f32[640,640]{0,1:T(8,128)} %get-tuple-element.20) | copy-start | bytes 4915204
  93.0 1.7 %copy-start.2 = (f32[640,1023]{0,1:T(8,128)S(1)}, f32[640,1023]{0,1:T(8,128)}, u32[]{:S(2)}) copy-start(f32[640,1023]{0,1:T(8,128)} %get-tuple-element.10) | copy-start | bytes 7856644
  96.4 5.0 %copy-start.5 = (bf16[1,1,1280,128]{3,2,1,0:T(8,128)(2,1)S(1)}, bf16[1,1,1280,128]{3,2,1,0:T(8,128)(2,1)}, u32[]{:S(2)}) copy-start(bf16[1,1,1280,128]{3,2,1,0:T(8,128)(2,1)} %param.5) | copy-start | bytes 983044
  98.0 3.4 %copy-start.1 = (f32[640,1280]{1,0:T(8,128)S(1)}, f32[640,1280]{1,0:T(8,128)}, u32[]{:S(2)}) copy-start(f32[640,1280]{1,0:T(8,128)} %get-tuple-element.16) | copy-start | bytes 9830404
  101.4 1.9 %copy-start = (f32[640,1280]{1,0:T(8,128)S(1)}, f32[640,1280]{1,0:T(8,128)}, u32[]{:S(2)}) copy-start(f32[640,1280]{1,0:T(8,128)} %get-tuple-element.8) | copy-start | bytes 9830404
where the time goes:
time: 107 us
  waiting for transfers between devices  53.6 us (50%)
  matrix products  22.6 us (21%)
  other arithmetic  13.1 us (12%)
  starting transfers between devices  11.5 us (11%)
  local copies, waits for them, and re-layouts  6 us (6%)
    ppermute x3, waiting for transfers between devices, passed_along(): return lax.ppermute(block, axis, route)  53.6 us
    dot_general x8, matrix products, masked_scores(): jnp.einsum('qd,kd->qk', query_tile, key_tile, preferred_element_type=jnp....  18.2 us
    ppermute x3, starting transfers between devices, passed_along(): return lax.ppermute(block, axis, route)  11.5 us
    reduce_sum x4, other arithmetic, joined_context(): row_total = jnp.sum(probable, axis=1, keepdims=True)  8.62 us
    dot_general x4, matrix products, joined_context(): jnp.dot(weights, value_tile, preferred_element_type=jnp.float32) / row_total  4.32 us
    select_n x2, local copies, waits for them, and re-layouts, masked_scores(): return jnp.where(valid, raw, -jnp.inf)  3.11 us
  transfers between devices with their start and end apart: 3, of which 2 were waited for; matrix products, arithmetic and copies ran while one was open for 12% of the time, Pallas kernels for 0%

commit v1 on v0

v1 whole, which is shorter than its diff:
```python
import functools

import jax
import jax.numpy as jnp
from jax import lax
from jax.experimental import pallas as pl
from jax.experimental.pallas import tpu as pltpu
from jax.sharding import PartitionSpec as P

KVH = 8
QPK = 2
WINDOW = 1024
QUERY_TILE = 256
LANES = 128


scale_factor = 168.0 ** (-0.5)


def tile_scores(query_tile, key_tile):
    raw = lax.dot_general(
        query_tile, key_tile, (((1,), (1,)), ((), ())), preferred_element_type=jnp.float32
    )
    return raw * scale_factor


def local_kernel(q_ref, k_ref, v_ref, out_ref, top_ref, total_ref, acc_ref):
    row_count = q_ref.shape[0]
    halo_rows = top_ref.shape[0]
    for first_row in range(0, row_count, QUERY_TILE):
        low_key = max(0, first_row - WINDOW + 1) // LANES * LANES
        high_key = first_row + QUERY_TILE
        scores = tile_scores(q_ref[first_row:high_key, :], k_ref[low_key:high_key, :])
        query_pos = first_row + lax.broadcasted_iota(jnp.int32, scores.shape, 0)
        key_pos = low_key + lax.broadcasted_iota(jnp.int32, scores.shape, 1)
        valid = (key_pos <= query_pos) & (query_pos - key_pos < WINDOW)
        scores = jnp.where(valid, scores, -jnp.inf)
        row_top = jnp.max(scores, axis=1, keepdims=True)
        probable = jnp.exp(scores - row_top)
        row_total = jnp.sum(probable, axis=1, keepdims=True)
        context = jnp.dot(
            probable.astype(jnp.bfloat16),
            v_ref[low_key:high_key, :],
            preferred_element_type=jnp.float32,
        )
        if first_row < halo_rows:
            top_ref[first_row:high_key, :] = jnp.broadcast_to(row_top, (QUERY_TILE, LANES))
            total_ref[first_row:high_key, :] = jnp.broadcast_to(row_total, (QUERY_TILE, LANES))
            acc_ref[first_row:high_key, :] = context
        else:
            out_ref[first_row:high_key, :] = (context / row_total).astype(out_ref.dtype)


def halo_kernel(opening_ref, q_ref, halo_ref, top_ref, total_ref, acc_ref, partial_ref, out_ref):
    halo_rows = top_ref.shape[0]
    window = halo_ref.shape[1]
    out_ref[halo_rows:, :] = partial_ref[halo_rows:, :]
    shut = opening_ref[0] != 0
    for first_row in range(0, halo_rows, QUERY_TILE):
        high_row = first_row + QUERY_TILE
        scores = tile_scores(q_ref[first_row:high_row, :], halo_ref[0, first_row:window, :])
        query_pos = first_row + lax.broadcasted_iota(jnp.int32, scores.shape, 0)
        key_pos = first_row + lax.broadcasted_iota(jnp.int32, scores.shape, 1)
        valid = (key_pos > query_pos) & jnp.logical_not(shut)
        scores = jnp.where(valid, scores, -jnp.inf)
        local_top = top_ref[first_row:high_row, 0:1]
        row_top = jnp.maximum(local_top, jnp.max(scores, axis=1, keepdims=True))
        probable = jnp.exp(scores - row_top)
        halo_total = jnp.sum(probable, axis=1, keepdims=True)
        halo_context = jnp.dot(
            probable.astype(jnp.bfloat16),
            halo_ref[1, first_row:window, :],
            preferred_element_type=jnp.float32,
        )
        rescale = jnp.exp(local_top - row_top)
        context = rescale * acc_ref[first_row:high_row, :] + halo_context
        row_total = rescale * total_ref[first_row:high_row, 0:1] + halo_total
        out_ref[first_row:high_row, :] = (context / row_total).astype(out_ref.dtype)


def local_part(query_local, key_local, value_local, halo_rows):
    row_count, width = query_local.shape
    head_size = key_local.shape[1]
    heads = width // head_size
    head_block = pl.BlockSpec((row_count, head_size), lambda p: (0, p))
    whole = pl.BlockSpec((row_count, head_size), lambda p: (0, 0))
    stat_block = pl.BlockSpec((None, halo_rows, LANES), lambda p: (p, 0, 0))
    acc_block = pl.BlockSpec((None, halo_rows, head_size), lambda p: (p, 0, 0))
    flops = 4 * heads * row_count * (WINDOW + QUERY_TILE) * head_size
    return pl.pallas_call(
        local_kernel,
        grid=(heads,),
        in_specs=[head_block, whole, whole],
        out_specs=[head_block, stat_block, stat_block, acc_block],
        out_shape=[
            jax.ShapeDtypeStruct((row_count, width), query_local.dtype),
            jax.ShapeDtypeStruct((heads, halo_rows, LANES), jnp.float32),
            jax.ShapeDtypeStruct((heads, halo_rows, LANES), jnp.float32),
            jax.ShapeDtypeStruct((heads, halo_rows, head_size), jnp.float32),
        ],
        cost_estimate=pl.CostEstimate(
            flops=flops,
            transcendentals=heads * row_count * (WINDOW + QUERY_TILE),
            bytes_accessed=4 * row_count * width + 12 * heads * halo_rows * LANES,
        ),
    )(query_local, key_local, value_local)


def halo_part(opening, query_local, halo, top, total, acc, partial_out):
    row_count, width = query_local.shape
    head_size = halo.shape[2]
    window = halo.shape[1]
    heads = width // head_size
    halo_rows = top.shape[1]
    query_block = pl.BlockSpec((row_count, head_size), lambda p, o: (0, p))
    halo_block = pl.BlockSpec((2, window, head_size), lambda p, o: (0, 0, 0))
    stat_block = pl.BlockSpec((None, halo_rows, LANES), lambda p, o: (p, 0, 0))
    acc_block = pl.BlockSpec((None, halo_rows, head_size), lambda p, o: (p, 0, 0))
    flops = 4 * heads * halo_rows * window * head_size
    return pl.pallas_call(
        halo_kernel,
        grid_spec=pltpu.PrefetchScalarGridSpec(
            num_scalar_prefetch=1,
            grid=(heads,),
            in_specs=[
                query_block,
                halo_block,
                stat_block,
                stat_block,
                acc_block,
                query_block,
            ],
            out_specs=query_block,
        ),
        out_shape=jax.ShapeDtypeStruct((row_count, width), partial_out.dtype),
        input_output_aliases={6: 0},
        cost_estimate=pl.CostEstimate(
            flops=flops,
            transcendentals=heads * halo_rows * window,
            bytes_accessed=3 * row_count * width * 2 + 12 * heads * halo_rows * LANES,
        ),
    )(opening, query_local, halo, top, total, acc, partial_out)


def per_device(queries, key_rows, value_rows):
    row_count = queries.shape[2]
    seq_count = lax.axis_size("seq")
    model_count = lax.axis_size("mp")
    blocks = model_count // KVH
    row_block = lax.axis_index("mp") // KVH
    opening = jnp.logical_and(lax.axis_index("seq") == 0, row_block == 0)
    opening = opening.astype(jnp.int32).reshape(1)
    query_local = queries[0, 0]
    key_local = key_rows[0, 0]
    value_local = value_rows[0, 0]
    halo_source = jnp.stack([key_local[row_count - WINDOW :], value_local[row_count - WINDOW :]])
    route = []
    for s in range(seq_count):
        for m in range(model_count):
            if m >= KVH:
                route.append((s * model_count + m - KVH, s * model_count + m))
            elif s > 0:
                route.append(((s - 1) * model_count + (blocks - 1) * KVH + m, s * model_count + m))
    halo = lax.ppermute(halo_source, ("seq", "mp"), route)
    halo_rows = -(-(WINDOW - 1) // QUERY_TILE) * QUERY_TILE
    partial_out, top, total, acc = local_part(query_local, key_local, value_local, halo_rows)
    attended = halo_part(opening, query_local, halo, top, total, acc, partial_out)
    return attended.reshape(1, 1, row_count, queries.shape[3])


def solution(mesh):
    in_specs = (P("seq", "mp", None, None), P("seq", "mp", None, None), P("seq", "mp", None, None))
    out_specs = P("seq", "mp", None, None)
    return jax.shard_map(
        per_device, mesh=mesh, in_specs=in_specs, out_specs=out_specs, check_vma=False
    )
```

time: 107 us -> 57.3 us (0.54)
  the two profiles are of different devices: /device:TPU:79 before, /device:TPU:6 now
where the time goes in v1:
time: 57.3 us; the launch traced here: 57.1 us
  waiting for transfers between devices  34.9 us (61%)
  Pallas kernels  14.2 us (25%)
  starting transfers between devices  6.09 us (11%)
  local copies, waits for them, and re-layouts  1.85 us (3%)
    ppermute x1, waiting for transfers between devices, per_device(): halo = lax.ppermute(halo_source, ('seq', 'mp'), route)  34.9 us
    pallas_call x1, Pallas kernels, halo_part(): pl.pallas_call(halo_kernel, grid_spec=pltpu.PrefetchScalarGridSpec(num_sc...  7.22 us
    pallas_call x1, Pallas kernels, local_part(): pl.pallas_call(local_kernel, grid=(heads,), in_specs=[head_block, whole,...  6.97 us
    ppermute x1, starting transfers between devices, per_device(): halo = lax.ppermute(halo_source, ('seq', 'mp'), route)  6.09 us
  transfers between devices with their start and end apart: 1, of which 1 were waited for; matrix products, arithmetic and copies ran while one was open for 0% of the time, Pallas kernels for 12%

profile of v1, /device:TPU:6, one launch (start us, length us, event | category | flops | bytes accessed | tf_op | source)
XLA Modules:
  0.0 57.1 jit_solution(10446266483605993987)
XLA Ops:
  0.0 1.1 %slice_bitcast_fusion = (bf16[1,1024,128]{2,1,0:T(8,128)(2,1)S(1)}, bf16[1,1024,128]{2,1,0:T(8,128)(2,1)S(1)}) fusion(bf16[1,1,1280,128]{3,2,1,0:T(8,128)(2,1)} %param.5, bf16[1,1,1280,128]{3,2,1,0:T(8,128)(2,1)} %param.4), kind=kLoop, calls=%fused_computation.1 | loop fusion | bytes 1048576 | tf_op jit(solution)/shard_map/stack | solution.py:156
  1.1 0.1 pad_maximum_fusion
  1.1 6.1 %collective-permute-start = (bf16[2,1024,128]{2,1,0:T(8,128)(2,1)S(1)}, bf16[2,1024,128]{2,1,0:T(8,128)(2,1)S(1)}, u32[]{:S(2)}, u32[]{:S(2)}) collective-permute-start(bf16[2,1024,128]{2,1,0:T(8,128)(2,1)S(1)} %pad_maximum_fusion), channel_id=1, source_target_pairs={{0,8},{1,9},{2,10},{3,11},{4,12},{5,13},{6,14},{7,15},{8,16},{9,17... | collective-permute-start | bytes 1572872 | tf_op jit(solution)/shard_map/ppermute | solution.py:164
  7.3 7.0 %shard_map.37 = (bf16[1280,256]{1,0:T(8,128)(2,1)}, f32[2,1024,128]{2,1,0:T(8,128)}, f32[2,1024,128]{2,1,0:T(8,128)}, f32[2,1024,128]{2,1,0:T(8,128)}) custom-call(bf16[1280,256]{1,0:T(8,128)(2,1)} %bitcast.9, bf16[1280,128]{1,0:T(8,128)(2,1)} %bitcast.12, bf16[1280,128]{1,0:T(8,128)(2,1)} %bitcast.11), custom_call_target="tpu_custom_call" | custom-call | flops 1677721600 | bytes 4456448 | tf_op jit(solution)/shard_map/pallas_call | solution.py:90
  14.2 34.9 %collective-permute-done.halo_ref = bf16[2,1024,128]{2,1,0:T(8,128)(2,1)S(1)} collective-permute-done((bf16[2,1024,128]{2,1,0:T(8,128)(2,1)S(1)}, bf16[2,1024,128]{2,1,0:T(8,128)(2,1)S(1)}, u32[]{:S(2)}, u32[]{:S(2)}) %collective-permute-start) | collective-permute-done | bytes 524320 | tf_op jit(solution)/shard_map/ppermute | solution.py:164
  49.1 0.0 copy-start
  49.1 0.8 %copy-done = bf16[2,1024,128]{2,1,0:T(8,128)(2,1)} copy-done((bf16[2,1024,128]{2,1,0:T(8,128)(2,1)}, bf16[2,1024,128]{2,1,0:T(8,128)(2,1)S(1)}, u32[]{:S(2)}) %copy-start) | copy-done | bytes 524312
  49.9 7.2 %shard_map.38 = bf16[1280,256]{1,0:T(8,128)(2,1)} custom-call(s32[1]{0:T(128)} %bitcast.opening_ref, bf16[1280,256]{1,0:T(8,128)(2,1)} %bitcast.10, bf16[2,1024,128]{2,1,0:T(8,128)(2,1)} %copy-done, f32[2,1024,128]{2,1,0:T(8,128)} %get-tuple-element.9.top_ref, f32[2,1024,128]{2,1,0:T(8,128)} %get-tuple-element.10.total_ref, ...), custom_call_target="tpu_custom_call", output_to_operand_aliasing={{}: (6, {})} | custom-call | flops 1073741824 | bytes 5111808 | tf_op jit(solution)/shard_map/pallas_call | solution.py:120
Async XLA Ops:
  1.1 48.0 %collective-permute-start = (bf16[2,1024,128]{2,1,0:T(8,128)(2,1)S(1)}, bf16[2,1024,128]{2,1,0:T(8,128)(2,1)S(1)}, u32[]{:S(2)}, u32[]{:S(2)}) collective-permute-start(bf16[2,1024,128]{2,1,0:T(8,128)(2,1)S(1)} %pad_maximum_fusion), channel_id=1, source_target_pairs={{0,8},{1,9},{2,10},{3,11},{4,12},{5,13},{6,14},{7,15},{8,16},{9,17... | collective-permute-start | bytes 1572872 | tf_op jit(solution)/shard_map/ppermute | solution.py:164
  49.1 0.8 %copy-start = (bf16[2,1024,128]{2,1,0:T(8,128)(2,1)}, bf16[2,1024,128]{2,1,0:T(8,128)(2,1)S(1)}, u32[]{:S(2)}) copy-start(bf16[2,1024,128]{2,1,0:T(8,128)(2,1)S(1)} %collective-permute-done.halo_ref) | copy-start | bytes 1572868

commit v2 on v1

v2 whole, which is shorter than its diff:
```python
import jax
import jax.numpy as jnp
from jax import lax
from jax.experimental import pallas as pl
from jax.experimental.pallas import tpu as pltpu
from jax.sharding import PartitionSpec as P

KVH = 8
QPK = 2
WINDOW = 1024
QUERY_TILE = 256
LANES = 128


scale_factor = 168.0 ** (-0.5)


def tile_scores(query_tile, key_tile):
    raw = lax.dot_general(
        query_tile, key_tile, (((1,), (1,)), ((), ())), preferred_element_type=jnp.float32
    )
    return raw * scale_factor


def packed_stats(row_top, row_total):
    lane = lax.broadcasted_iota(jnp.int32, (row_top.shape[0], LANES), 1)
    return jnp.where(lane < LANES // 2, row_top, row_total)


def local_kernel(q_ref, k_ref, v_ref, out_ref, stats_ref, acc_ref):
    row_count = q_ref.shape[0]
    halo_rows = stats_ref.shape[0]
    for first_row in range(0, row_count, QUERY_TILE):
        low_key = max(0, first_row - WINDOW + 1) // LANES * LANES
        high_key = first_row + QUERY_TILE
        scores = tile_scores(q_ref[first_row:high_key, :], k_ref[low_key:high_key, :])
        query_pos = first_row + lax.broadcasted_iota(jnp.int32, scores.shape, 0)
        key_pos = low_key + lax.broadcasted_iota(jnp.int32, scores.shape, 1)
        valid = (key_pos <= query_pos) & (query_pos - key_pos < WINDOW)
        scores = jnp.where(valid, scores, -jnp.inf)
        row_top = jnp.max(scores, axis=1, keepdims=True)
        probable = jnp.exp(scores - row_top)
        row_total = jnp.sum(probable, axis=1, keepdims=True)
        context = jnp.dot(
            probable.astype(jnp.bfloat16),
            v_ref[low_key:high_key, :],
            preferred_element_type=jnp.float32,
        )
        if first_row < halo_rows:
            stats_ref[first_row:high_key, :] = packed_stats(row_top, row_total)
            acc_ref[first_row:high_key, :] = context
        else:
            out_ref[first_row:high_key, :] = (context / row_total).astype(out_ref.dtype)


def halo_tile(first_row, shut, q_ref, halo_ref, stats_ref, acc_ref, out_ref):
    window = halo_ref.shape[1]
    query_tile = q_ref[...]
    near_row = first_row + QUERY_TILE
    near = tile_scores(query_tile, halo_ref[0, first_row:near_row, :])
    above = lax.broadcasted_iota(jnp.int32, near.shape, 1) > lax.broadcasted_iota(
        jnp.int32, near.shape, 0
    )
    near = jnp.where(above, near, -jnp.inf)
    parts = [(near, halo_ref[1, first_row:near_row, :])]
    if near_row < window:
        far = tile_scores(query_tile, halo_ref[0, near_row:window, :])
        parts.append((far, halo_ref[1, near_row:window, :]))
    local_top = stats_ref[:, 0:1]
    local_total = stats_ref[:, LANES // 2 : LANES // 2 + 1]
    local_context = acc_ref[...]
    row_top = local_top
    for scores, _ in parts:
        row_top = jnp.maximum(row_top, jnp.max(scores, axis=1, keepdims=True))
    rescale = jnp.exp(local_top - row_top)
    context = rescale * local_context
    row_total = rescale * local_total
    for scores, values in parts:
        probable = jnp.exp(scores - row_top)
        row_total = row_total + jnp.sum(probable, axis=1, keepdims=True)
        context = context + jnp.dot(
            probable.astype(jnp.bfloat16), values, preferred_element_type=jnp.float32
        )
    joined = context / row_total
    alone = local_context / local_total
    out_ref[...] = jnp.where(shut, alone, joined).astype(out_ref.dtype)


def halo_kernel(opening_ref, q_ref, halo_ref, stats_ref, acc_ref, _, out_ref):
    tile = pl.program_id(1)
    shut = opening_ref[0] != 0
    for index in range(pl.num_programs(1)):

        @pl.when(tile == index)
        def _():
            halo_tile(index * QUERY_TILE, shut, q_ref, halo_ref, stats_ref, acc_ref, out_ref)


def local_part(query_local, key_local, value_local, halo_rows):
    row_count, width = query_local.shape
    head_size = key_local.shape[1]
    heads = width // head_size
    head_block = pl.BlockSpec((row_count, head_size), lambda p: (0, p))
    whole = pl.BlockSpec((row_count, head_size), lambda p: (0, 0))
    stat_block = pl.BlockSpec((None, halo_rows, LANES), lambda p: (p, 0, 0))
    acc_block = pl.BlockSpec((None, halo_rows, head_size), lambda p: (p, 0, 0))
    flops = 4 * heads * row_count * (WINDOW + QUERY_TILE) * head_size
    return pl.pallas_call(
        local_kernel,
        grid=(heads,),
        in_specs=[head_block, whole, whole],
        out_specs=[head_block, stat_block, acc_block],
        out_shape=[
            jax.ShapeDtypeStruct((row_count, width), query_local.dtype),
            jax.ShapeDtypeStruct((heads, halo_rows, LANES), jnp.float32),
            jax.ShapeDtypeStruct((heads, halo_rows, head_size), jnp.float32),
        ],
        cost_estimate=pl.CostEstimate(
            flops=flops,
            transcendentals=heads * row_count * (WINDOW + QUERY_TILE),
            bytes_accessed=4 * row_count * width + 8 * heads * halo_rows * LANES,
        ),
    )(query_local, key_local, value_local)


def halo_part(opening, query_local, halo, stats, acc, partial_out):
    row_count, width = query_local.shape
    head_size = halo.shape[2]
    window = halo.shape[1]
    heads = width // head_size
    halo_rows = stats.shape[1]
    tiles = halo_rows // QUERY_TILE
    query_block = pl.BlockSpec((QUERY_TILE, head_size), lambda p, i, o: (i, p))
    stat_block = pl.BlockSpec((None, QUERY_TILE, LANES), lambda p, i, o: (p, i, 0))
    acc_block = pl.BlockSpec((None, QUERY_TILE, head_size), lambda p, i, o: (p, i, 0))
    flops = 2 * heads * halo_rows * window * head_size
    return pl.pallas_call(
        halo_kernel,
        grid_spec=pltpu.PrefetchScalarGridSpec(
            num_scalar_prefetch=1,
            grid=(heads, tiles),
            in_specs=[
                query_block,
                pl.BlockSpec(memory_space=pltpu.VMEM),
                stat_block,
                acc_block,
                pl.BlockSpec(memory_space=pl.ANY),
            ],
            out_specs=query_block,
        ),
        out_shape=jax.ShapeDtypeStruct((row_count, width), partial_out.dtype),
        input_output_aliases={5: 0},
        cost_estimate=pl.CostEstimate(
            flops=flops,
            transcendentals=heads * halo_rows * window // 2,
            bytes_accessed=2 * halo_rows * width * 2 + 8 * heads * halo_rows * LANES,
        ),
    )(opening, query_local, halo, stats, acc, partial_out)


def per_device(queries, key_rows, value_rows):
    row_count = queries.shape[2]
    seq_count = lax.axis_size("seq")
    model_count = lax.axis_size("mp")
    blocks = model_count // KVH
    row_block = lax.axis_index("mp") // KVH
    opening = jnp.logical_and(lax.axis_index("seq") == 0, row_block == 0)
    opening = opening.astype(jnp.int32).reshape(1)
    query_local = queries[0, 0]
    key_local = key_rows[0, 0]
    value_local = value_rows[0, 0]
    halo_source = jnp.stack([key_local[row_count - WINDOW :], value_local[row_count - WINDOW :]])
    route = []
    for s in range(seq_count):
        for m in range(model_count):
            if m >= KVH:
                route.append((s * model_count + m - KVH, s * model_count + m))
            elif s > 0:
                route.append(((s - 1) * model_count + (blocks - 1) * KVH + m, s * model_count + m))
    halo = lax.ppermute(halo_source, ("seq", "mp"), route)
    halo_rows = -(-(WINDOW - 1) // QUERY_TILE) * QUERY_TILE
    partial_out, stats, acc = local_part(query_local, key_local, value_local, halo_rows)
    attended = halo_part(opening, query_local, halo, stats, acc, partial_out)
    return attended.reshape(1, 1, row_count, queries.shape[3])


def solution(mesh):
    in_specs = (P("seq", "mp", None, None), P("seq", "mp", None, None), P("seq", "mp", None, None))
    out_specs = P("seq", "mp", None, None)
    return jax.shard_map(
        per_device, mesh=mesh, in_specs=in_specs, out_specs=out_specs, check_vma=False
    )
```

time: 57.3 us -> 58.8 us (1.026)
  Pallas kernels: 14.2 us -> 15.6 us
    pallas_call x1, Pallas kernels: 7.22 us -> 8.62 us  [halo_part(): pl.pallas_call(halo_kernel, grid_spec=pltpu.PrefetchScalarGridSpec(num_sc...]
where the time goes in v2:
time: 58.8 us; the launch traced here: 58.5 us
  waiting for transfers between devices  34.8 us (59%)
  Pallas kernels  15.6 us (27%)
  starting transfers between devices  6.09 us (10%)
  local copies, waits for them, and re-layouts  1.86 us (3%)
    ppermute x1, waiting for transfers between devices, per_device(): halo = lax.ppermute(halo_source, ('seq', 'mp'), route)  34.8 us
    pallas_call x1, Pallas kernels, halo_part(): pl.pallas_call(halo_kernel, grid_spec=pltpu.PrefetchScalarGridSpec(num_sc...  8.62 us
    pallas_call x1, Pallas kernels, local_part(): pl.pallas_call(local_kernel, grid=(heads,), in_specs=[head_block, whole,...  7.03 us
    ppermute x1, starting transfers between devices, per_device(): halo = lax.ppermute(halo_source, ('seq', 'mp'), route)  6.09 us
  transfers between devices with their start and end apart: 1, of which 1 were waited for; matrix products, arithmetic and copies ran while one was open for 0% of the time, Pallas kernels for 12%

profile of v2, /device:TPU:6, one launch (start us, length us, event | category | flops | bytes accessed | tf_op | source)
XLA Modules:
  0.0 58.5 jit_solution(190031783699059819)
XLA Ops:
  0.0 1.1 %slice_bitcast_fusion = (bf16[1,1024,128]{2,1,0:T(8,128)(2,1)S(1)}, bf16[1,1024,128]{2,1,0:T(8,128)(2,1)S(1)}) fusion(bf16[1,1,1280,128]{3,2,1,0:T(8,128)(2,1)} %param.5, bf16[1,1,1280,128]{3,2,1,0:T(8,128)(2,1)} %param.4), kind=kLoop, calls=%fused_computation.1 | loop fusion | bytes 1048576 | tf_op jit(solution)/shard_map/stack | solution.py:172
  1.1 0.1 pad_maximum_fusion
  1.1 6.1 %collective-permute-start = (bf16[2,1024,128]{2,1,0:T(8,128)(2,1)S(1)}, bf16[2,1024,128]{2,1,0:T(8,128)(2,1)S(1)}, u32[]{:S(2)}, u32[]{:S(2)}) collective-permute-start(bf16[2,1024,128]{2,1,0:T(8,128)(2,1)S(1)} %pad_maximum_fusion), channel_id=1, source_target_pairs={{0,8},{1,9},{2,10},{3,11},{4,12},{5,13},{6,14},{7,15},{8,16},{9,17... | collective-permute-start | bytes 1572872 | tf_op jit(solution)/shard_map/ppermute | solution.py:180
  7.3 7.0 %shard_map.37 = (bf16[1280,256]{1,0:T(8,128)(2,1)}, f32[2,1024,128]{2,1,0:T(8,128)}, f32[2,1024,128]{2,1,0:T(8,128)}) custom-call(bf16[1280,256]{1,0:T(8,128)(2,1)} %bitcast.9, bf16[1280,128]{1,0:T(8,128)(2,1)} %bitcast.12, bf16[1280,128]{1,0:T(8,128)(2,1)} %bitcast.11), custom_call_target="tpu_custom_call" | custom-call | flops 1677721600 | bytes 3407872 | tf_op jit(solution)/shard_map/pallas_call | solution.py:108
  14.3 34.8 %collective-permute-done.halo_ref = bf16[2,1024,128]{2,1,0:T(8,128)(2,1)S(1)} collective-permute-done((bf16[2,1024,128]{2,1,0:T(8,128)(2,1)S(1)}, bf16[2,1024,128]{2,1,0:T(8,128)(2,1)S(1)}, u32[]{:S(2)}, u32[]{:S(2)}) %collective-permute-start) | collective-permute-done | bytes 524320 | tf_op jit(solution)/shard_map/ppermute | solution.py:180
  49.1 0.0 copy-start
  49.1 0.8 %copy-done = bf16[2,1024,128]{2,1,0:T(8,128)(2,1)} copy-done((bf16[2,1024,128]{2,1,0:T(8,128)(2,1)}, bf16[2,1024,128]{2,1,0:T(8,128)(2,1)S(1)}, u32[]{:S(2)}) %copy-start) | copy-done | bytes 524312
  49.9 8.6 %shard_map.38 = bf16[1280,256]{1,0:T(8,128)(2,1)} custom-call(s32[1]{0:T(128)} %bitcast.opening_ref, bf16[1280,256]{1,0:T(8,128)(2,1)} %bitcast.10, bf16[2,1024,128]{2,1,0:T(8,128)(2,1)} %copy-done, f32[2,1024,128]{2,1,0:T(8,128)} %get-tuple-element.8.stats_ref, f32[2,1024,128]{2,1,0:T(8,128)} %get-tuple-element.9.acc_ref, ...), custom_call_target="tpu_custom_call", output_to_operand_aliasing={{}: (5, {})} | custom-call | flops 536870912 | bytes 3145728 | tf_op jit(solution)/shard_map/pallas_call | solution.py:137
Async XLA Ops:
  1.1 48.0 %collective-permute-start = (bf16[2,1024,128]{2,1,0:T(8,128)(2,1)S(1)}, bf16[2,1024,128]{2,1,0:T(8,128)(2,1)S(1)}, u32[]{:S(2)}, u32[]{:S(2)}) collective-permute-start(bf16[2,1024,128]{2,1,0:T(8,128)(2,1)S(1)} %pad_maximum_fusion), channel_id=1, source_target_pairs={{0,8},{1,9},{2,10},{3,11},{4,12},{5,13},{6,14},{7,15},{8,16},{9,17... | collective-permute-start | bytes 1572872 | tf_op jit(solution)/shard_map/ppermute | solution.py:180
  49.1 0.8 %copy-start = (bf16[2,1024,128]{2,1,0:T(8,128)(2,1)}, bf16[2,1024,128]{2,1,0:T(8,128)(2,1)S(1)}, u32[]{:S(2)}) copy-start(bf16[2,1024,128]{2,1,0:T(8,128)(2,1)S(1)} %collective-permute-done.halo_ref) | copy-start | bytes 1572868

commit v3 on v2

--- a/solution.py
+++ b/solution.py
@@ -53,22 +53,22 @@
             out_ref[first_row:high_key, :] = (context / row_total).astype(out_ref.dtype)
 
 
-def halo_tile(first_row, shut, q_ref, halo_ref, stats_ref, acc_ref, out_ref):
-    window = halo_ref.shape[1]
-    query_tile = q_ref[...]
-    near_row = first_row + QUERY_TILE
-    near = tile_scores(query_tile, halo_ref[0, first_row:near_row, :])
-    above = lax.broadcasted_iota(jnp.int32, near.shape, 1) > lax.broadcasted_iota(
-        jnp.int32, near.shape, 0
-    )
-    near = jnp.where(above, near, -jnp.inf)
-    parts = [(near, halo_ref[1, first_row:near_row, :])]
-    if near_row < window:
-        far = tile_scores(query_tile, halo_ref[0, near_row:window, :])
-        parts.append((far, halo_ref[1, near_row:window, :]))
-    local_top = stats_ref[:, 0:1]
-    local_total = stats_ref[:, LANES // 2 : LANES // 2 + 1]
-    local_context = acc_ref[...]
+def merge_tile(query_tile, chunk_ref, offset, first_row, low_key, high_key, local):
+    parts = []
+    far_key = low_key
+    if first_row >= low_key:
+        near_row = first_row + QUERY_TILE
+        near = tile_scores(query_tile, chunk_ref[0, first_row - offset : near_row - offset, :])
+        above = lax.broadcasted_iota(jnp.int32, near.shape, 1) > lax.broadcasted_iota(
+            jnp.int32, near.shape, 0
+        )
+        near = jnp.where(above, near, -jnp.inf)
+        parts.append((near, chunk_ref[1, first_row - offset : near_row - offset, :]))
+        far_key = near_row
+    if far_key < high_key:
+        far = tile_scores(query_tile, chunk_ref[0, far_key - offset : high_key - offset, :])
+        parts.append((far, chunk_ref[1, far_key - offset : high_key - offset, :]))
+    local_top, local_total, local_context = local
     row_top = local_top
     for scores, _ in parts:
         row_top = jnp.maximum(row_top, jnp.max(scores, axis=1, keepdims=True))
@@ -81,19 +81,56 @@
         context = context + jnp.dot(
             probable.astype(jnp.bfloat16), values, preferred_element_type=jnp.float32
         )
-    joined = context / row_total
-    alone = local_context / local_total
-    out_ref[...] = jnp.where(shut, alone, joined).astype(out_ref.dtype)
-
-
-def halo_kernel(opening_ref, q_ref, halo_ref, stats_ref, acc_ref, _, out_ref):
-    tile = pl.program_id(1)
+    return row_top, row_total, context
+
+
+def read_stats(stats_ref, acc_ref, first_row):
+    high_row = first_row + QUERY_TILE
+    return (
+        stats_ref[first_row:high_row, 0:1],
+        stats_ref[first_row:high_row, LANES // 2 : LANES // 2 + 1],
+        acc_ref[first_row:high_row, :],
+    )
+
+
+def finish(shut, local, merged):
+    joined = merged[2] / merged[1]
+    alone = local[2] / local[1]
+    return jnp.where(shut, alone, joined)
+
+
+def far_kernel(
+    opening_ref, q_ref, chunk_ref, stats_ref, acc_ref, partial_ref, out_ref, open_stats, open_acc
+):
+    halo_rows = stats_ref.shape[0]
+    offset = halo_rows - chunk_ref.shape[1]
     shut = opening_ref[0] != 0
-    for index in range(pl.num_programs(1)):
-
-        @pl.when(tile == index)
-        def _():
-            halo_tile(index * QUERY_TILE, shut, q_ref, halo_ref, stats_ref, acc_ref, out_ref)
+    out_ref[halo_rows:, :] = partial_ref[halo_rows:, :]
+    for first_row in range(0, halo_rows, QUERY_TILE):
+        high_row = first_row + QUERY_TILE
+        local = read_stats(stats_ref, acc_ref, first_row)
+        merged = merge_tile(
+            q_ref[first_row:high_row, :], chunk_ref, offset, first_row, max(first_row, offset),
+            halo_rows, local,
+        )
+        if first_row >= offset:
+            out_ref[first_row:high_row, :] = finish(shut, local, merged).astype(out_ref.dtype)
+        else:
+            kept = [jnp.where(shut, a, b) for a, b in zip(local, merged)]
+            open_stats[first_row:high_row, :] = packed_stats(kept[0], kept[1])
+            open_acc[first_row:high_row, :] = kept[2]
+
+
+def near_kernel(opening_ref, q_ref, chunk_ref, stats_ref, acc_ref, _, out_ref):
+    open_rows = stats_ref.shape[0]
+    shut = opening_ref[0] != 0
+    for first_row in range(0, open_rows, QUERY_TILE):
+        high_row = first_row + QUERY_TILE
+        local = read_stats(stats_ref, acc_ref, first_row)
+        merged = merge_tile(
+            q_ref[first_row:high_row, :], chunk_ref, 0, first_row, first_row, open_rows, local
+        )
+        out_ref[first_row:high_row, :] = finish(shut, local, merged).astype(out_ref.dtype)
 
 
 def local_part(query_local, key_local, value_local, halo_rows):
@@ -123,25 +160,60 @@
     )(query_local, key_local, value_local)
 
 
-def halo_part(opening, query_local, halo, stats, acc, partial_out):
+def far_part(opening, query_local, chunk, stats, acc, partial_out):
     row_count, width = query_local.shape
-    head_size = halo.shape[2]
-    window = halo.shape[1]
+    head_size = chunk.shape[2]
+    chunk_rows = chunk.shape[1]
     heads = width // head_size
     halo_rows = stats.shape[1]
-    tiles = halo_rows // QUERY_TILE
-    query_block = pl.BlockSpec((QUERY_TILE, head_size), lambda p, i, o: (i, p))
-    stat_block = pl.BlockSpec((None, QUERY_TILE, LANES), lambda p, i, o: (p, i, 0))
-    acc_block = pl.BlockSpec((None, QUERY_TILE, head_size), lambda p, i, o: (p, i, 0))
-    flops = 2 * heads * halo_rows * window * head_size
+    open_rows = halo_rows - chunk_rows
+    column = pl.BlockSpec((row_count, head_size), lambda p, o: (0, p))
+    chunk_block = pl.BlockSpec(chunk.shape, lambda p, o: (0, 0, 0))
+    stat_block = pl.BlockSpec((None, halo_rows, LANES), lambda p, o: (p, 0, 0))
+    acc_block = pl.BlockSpec((None, halo_rows, head_size), lambda p, o: (p, 0, 0))
+    open_stat_block = pl.BlockSpec((None, open_rows, LANES), lambda p, o: (p, 0, 0))
+    open_acc_block = pl.BlockSpec((None, open_rows, head_size), lambda p, o: (p, 0, 0))
+    flops = 2 * heads * halo_rows * chunk_rows * head_size
     return pl.pallas_call(
-        halo_kernel,
+        far_kernel,
         grid_spec=pltpu.PrefetchScalarGridSpec(
             num_scalar_prefetch=1,
-            grid=(heads, tiles),
+            grid=(heads,),
+            in_specs=[column, chunk_block, stat_block, acc_block, column],
+            out_specs=[column, open_stat_block, open_acc_block],
+        ),
+        out_shape=[
+            jax.ShapeDtypeStruct((row_count, width), partial_out.dtype),
+            jax.ShapeDtypeStruct((heads, open_rows, LANES), jnp.float32),
+            jax.ShapeDtypeStruct((heads, open_rows, head_size), jnp.float32),
+        ],
+        input_output_aliases={5: 0},
+        cost_estimate=pl.CostEstimate(
+            flops=flops,
+            transcendentals=heads * halo_rows * chunk_rows // 2,
+            bytes_accessed=3 * row_count * width * 2 + 8 * heads * halo_rows * LANES,
+        ),
+    )(opening, query_local, chunk, stats, acc, partial_out)
+
+
+def near_part(opening, query_local, chunk, stats, acc, partial_out):
+    row_count, width = query_local.shape
+    head_size = chunk.shape[2]
+    heads = width // head_size
+    open_rows = stats.shape[1]
+    query_block = pl.BlockSpec((open_rows, head_size), lambda p, o: (0, p))
+    chunk_block = pl.BlockSpec(chunk.shape, lambda p, o: (0, 0, 0))
+    stat_block = pl.BlockSpec((None, open_rows, LANES), lambda p, o: (p, 0, 0))
+    acc_block = pl.BlockSpec((None, open_rows, head_size), lambda p, o: (p, 0, 0))
+    flops = 2 * heads * open_rows * open_rows * head_size
+    return pl.pallas_call(
+        near_kernel,
+        grid_spec=pltpu.PrefetchScalarGridSpec(
+            num_scalar_prefetch=1,
+            grid=(heads,),
             in_specs=[
                 query_block,
-                pl.BlockSpec(memory_space=pltpu.VMEM),
+                chunk_block,
                 stat_block,
                 acc_block,
                 pl.BlockSpec(memory_space=pl.ANY),
@@ -152,10 +224,10 @@
         input_output_aliases={5: 0},
         cost_estimate=pl.CostEstimate(
             flops=flops,
-            transcendentals=heads * halo_rows * window // 2,
-            bytes_accessed=2 * halo_rows * width * 2 + 8 * heads * halo_rows * LANES,
-        ),
-    )(opening, query_local, halo, stats, acc, partial_out)
+            transcendentals=heads * open_rows * open_rows,
+            bytes_accessed=2 * open_rows * width * 2 + 8 * heads * open_rows * LANES,
+        ),
+    )(opening, query_local, chunk, stats, acc, partial_out)
 
 
 def per_device(queries, key_rows, value_rows):
@@ -169,7 +241,11 @@
     query_local = queries[0, 0]
     key_local = key_rows[0, 0]
     value_local = value_rows[0, 0]
-    halo_source = jnp.stack([key_local[row_count - WINDOW :], value_local[row_count - WINDOW :]])
+    split_row = row_count - WINDOW + QUERY_TILE
+    far_source = jnp.stack([key_local[split_row:], value_local[split_row:]])
+    near_source = jnp.stack(
+        [key_local[row_count - WINDOW : split_row], value_local[row_count - WINDOW : split_row]]
+    )
     route = []
     for s in range(seq_count):
         for m in range(model_count):
@@ -177,10 +253,14 @@
                 route.append((s * model_count + m - KVH, s * model_count + m))
             elif s > 0:
                 route.append(((s - 1) * model_count + (blocks - 1) * KVH + m, s * model_count + m))
-    halo = lax.ppermute(halo_source, ("seq", "mp"), route)
-    halo_rows = -(-(WINDOW - 1) // QUERY_TILE) * QUERY_TILE
+    far_chunk = lax.ppermute(far_source, ("seq", "mp"), route)
+    near_chunk = lax.ppermute(near_source, ("seq", "mp"), route)
+    halo_rows = WINDOW
     partial_out, stats, acc = local_part(query_local, key_local, value_local, halo_rows)
-    attended = halo_part(opening, query_local, halo, stats, acc, partial_out)
+    partial_out, open_stats, open_acc = far_part(
+        opening, query_local, far_chunk, stats, acc, partial_out
+    )
+    attended = near_part(opening, query_local, near_chunk, open_stats, open_acc, partial_out)
     return attended.reshape(1, 1, row_count, queries.shape[3])
 
 

time: 58.8 us -> 58 us (0.986)
  waiting for transfers between devices: 34.8 us -> 24.2 us
  starting transfers between devices: 6.09 us -> 13.4 us
  local copies, waits for them, and re-layouts: 1.86 us -> 3.32 us
  Pallas kernels: 15.6 us -> 16.6 us
    ppermute x1 -> x2, waiting for transfers between devices: 34.8 us -> 24.2 us  [the longest x1 24.2 us: per_device(): far_chunk = lax.ppermute(far_source, ('seq', 'mp'), route)]
    ppermute x1 -> x2, starting transfers between devices: 6.09 us -> 13.4 us  [the longest x1 7.3 us: per_device(): near_chunk = lax.ppermute(near_source, ('seq', 'mp'), route)]
    pallas_call x1 -> x2, Pallas kernels: 8.62 us -> 9.59 us  [the longest x1 6.72 us: far_part(): pl.pallas_call(far_kernel, grid_spec=pltpu.PrefetchScalarGridSpec(num_sca...]
    another operation x1 -> x2, local copies, waits for them, and re-layouts: 1.06 us -> 1.93 us  [the longest x1 1.05 us: per_device(): far_source = jnp.stack([key_local[split_row:], value_local[split_row:]])]
    unnamed x2 -> x4, local copies, waits for them, and re-layouts: 0.8 us -> 1.39 us
  transfers between devices with their start and end apart: 1 -> 2, of which waited for: 1 -> 1; matrix products, arithmetic and copies ran while one was open for 0% -> 2% of each run, Pallas kernels for 12% -> 24%
where the time goes in v3:
time: 58 us; the launch traced here: 57.7 us
  waiting for transfers between devices  24.2 us (42%)
  Pallas kernels  16.6 us (29%)
  starting transfers between devices  13.4 us (23%)
  local copies, waits for them, and re-layouts  3.32 us (6%)
    ppermute x1, waiting for transfers between devices, per_device(): far_chunk = lax.ppermute(far_source, ('seq', 'mp'), route)  24.2 us
    ppermute x1, starting transfers between devices, per_device(): near_chunk = lax.ppermute(near_source, ('seq', 'mp'), route)  7.3 us
    pallas_call x1, Pallas kernels, local_part(): pl.pallas_call(local_kernel, grid=(heads,), in_specs=[head_block, whole,...  7.03 us
    pallas_call x1, Pallas kernels, far_part(): pl.pallas_call(far_kernel, grid_spec=pltpu.PrefetchScalarGridSpec(num_sca...  6.72 us
    ppermute x1, starting transfers between devices, per_device(): far_chunk = lax.ppermute(far_source, ('seq', 'mp'), route)  6.09 us
    pallas_call x1, Pallas kernels, near_part(): pl.pallas_call(near_kernel, grid_spec=pltpu.PrefetchScalarGridSpec(num_sc...  2.86 us
    unnamed x4, local copies, waits for them, and re-layouts  1.39 us
  transfers between devices with their start and end apart: 2, of which 1 were waited for; matrix products, arithmetic and copies ran while one was open for 2% of the time, Pallas kernels for 24%

profile of v3, /device:TPU:6, one launch (start us, length us, event | category | flops | bytes accessed | tf_op | source)
XLA Modules:
  0.0 57.7 jit_solution(1431795133398040710)
XLA Ops:
  0.0 1.0 %slice_bitcast_fusion = (bf16[1,768,128]{2,1,0:T(8,128)(2,1)S(1)}, bf16[1,768,128]{2,1,0:T(8,128)(2,1)S(1)}) fusion(bf16[1,1,1280,128]{3,2,1,0:T(8,128)(2,1)} %param.5, bf16[1,1,1280,128]{3,2,1,0:T(8,128)(2,1)} %param.4), kind=kLoop, calls=%fused_computation.1 | loop fusion | bytes 786432 | tf_op jit(solution)/shard_map/stack | solution.py:245
  1.1 6.1 %collective-permute-start.1 = (bf16[2,768,128]{2,1,0:T(8,128)(2,1)S(1)}, bf16[2,768,128]{2,1,0:T(8,128)(2,1)S(1)}, u32[]{:S(2)}, u32[]{:S(2)}) collective-permute-start(bf16[2,768,128]{2,1,0:T(8,128)(2,1)S(1)} %pad_maximum_fusion), channel_id=1, source_target_pairs={{0,8},{1,9},{2,10},{3,11},{4,12},{5,13},{6,14},{7,15},{8,16},{9,17... | collective-permute-start | bytes 1179656 | tf_op jit(solution)/shard_map/ppermute | solution.py:256
  7.2 0.9 %slice_bitcast_fusion.2 = (bf16[1,256,128]{2,1,0:T(8,128)(2,1)S(1)}, bf16[1,256,128]{2,1,0:T(8,128)(2,1)S(1)}) fusion(bf16[1,1,1280,128]{3,2,1,0:T(8,128)(2,1)} %param.5, bf16[1,1,1280,128]{3,2,1,0:T(8,128)(2,1)} %param.4), kind=kLoop, calls=%fused_computation.4 | loop fusion | bytes 262144 | tf_op jit(solution)/shard_map/stack | solution.py:246
  8.1 7.3 %collective-permute-start = (bf16[2,256,128]{2,1,0:T(8,128)(2,1)S(1)}, bf16[2,256,128]{2,1,0:T(8,128)(2,1)S(1)}, u32[]{:S(2)}, u32[]{:S(2)}) collective-permute-start(bf16[2,256,128]{2,1,0:T(8,128)(2,1)S(1)} %pad_maximum_fusion.1), channel_id=1, source_target_pairs={{0,8},{1,9},{2,10},{3,11},{4,12},{5,13},{6,14},{7,15},{8,16},{9,17... | collective-permute-start | bytes 393224 | tf_op jit(solution)/shard_map/ppermute | solution.py:257
  15.5 7.0 %shard_map.37 = (bf16[1280,256]{1,0:T(8,128)(2,1)}, f32[2,1024,128]{2,1,0:T(8,128)}, f32[2,1024,128]{2,1,0:T(8,128)}) custom-call(bf16[1280,256]{1,0:T(8,128)(2,1)} %bitcast.13, bf16[1280,128]{1,0:T(8,128)(2,1)} %bitcast.17, bf16[1280,128]{1,0:T(8,128)(2,1)} %bitcast.16), custom_call_target="tpu_custom_call" | custom-call | flops 1677721600 | bytes 3407872 | tf_op jit(solution)/shard_map/pallas_call | solution.py:145
  22.5 24.2 %collective-permute-done.1.chunk_ref = bf16[2,768,128]{2,1,0:T(8,128)(2,1)S(1)} collective-permute-done((bf16[2,768,128]{2,1,0:T(8,128)(2,1)S(1)}, bf16[2,768,128]{2,1,0:T(8,128)(2,1)S(1)}, u32[]{:S(2)}, u32[]{:S(2)}) %collective-permute-start.1) | collective-permute-done | bytes 393248 | tf_op jit(solution)/shard_map/ppermute | solution.py:256
  46.7 0.0 copy-start
  46.7 0.7 %copy-done = bf16[2,768,128]{2,1,0:T(8,128)(2,1)} copy-done((bf16[2,768,128]{2,1,0:T(8,128)(2,1)}, bf16[2,768,128]{2,1,0:T(8,128)(2,1)S(1)}, u32[]{:S(2)}) %copy-start) | copy-done | bytes 393240
  47.5 6.7 %shard_map.38 = (bf16[1280,256]{1,0:T(8,128)(2,1)}, f32[2,256,128]{2,1,0:T(8,128)}, f32[2,256,128]{2,1,0:T(8,128)}) custom-call(s32[1]{0:T(128)} %bitcast.opening_ref, bf16[1280,256]{1,0:T(8,128)(2,1)} %bitcast.14, bf16[2,768,128]{2,1,0:T(8,128)(2,1)} %copy-done, f32[2,1024,128]{2,1,0:T(8,128)} %get-tuple-element.11.stats_ref, ...), custom_call_target="tpu_custom_call", output_to_operand_aliasing={{0}: (5, {})} | custom-call | flops 402653184 | bytes 4063232 | tf_op jit(solution)/shard_map/pallas_call | solution.py:177
  54.2 0.0 collective-permute-done.chunk_ref
  54.2 0.0 copy-start.1
  54.2 0.6 %copy-done.1 = bf16[2,256,128]{2,1,0:T(8,128)(2,1)} copy-done((bf16[2,256,128]{2,1,0:T(8,128)(2,1)}, bf16[2,256,128]{2,1,0:T(8,128)(2,1)S(1)}, u32[]{:S(2)}) %copy-start.1) | copy-done | bytes 131096
  54.8 2.9 %shard_map.39 = bf16[1280,256]{1,0:T(8,128)(2,1)} custom-call(s32[1]{0:T(128)} %bitcast.opening_ref, bf16[1280,256]{1,0:T(8,128)(2,1)} %bitcast.15, bf16[2,256,128]{2,1,0:T(8,128)(2,1)} %copy-done.1, f32[2,256,128]{2,1,0:T(8,128)} %get-tuple-element.14.stats_ref, f32[2,256,128]{2,1,0:T(8,128)} %get-tuple-element.15.acc_ref, ...), custom_call_target="tpu_custom_call", output_to_operand_aliasing={{}: (5, {})} | custom-call | flops 33554432 | bytes 786432 | tf_op jit(solution)/shard_map/pallas_call | solution.py:209
  (2 shorter events, 0.1 us)
Async XLA Ops:
  1.1 45.6 %collective-permute-start.1 = (bf16[2,768,128]{2,1,0:T(8,128)(2,1)S(1)}, bf16[2,768,128]{2,1,0:T(8,128)(2,1)S(1)}, u32[]{:S(2)}, u32[]{:S(2)}) collective-permute-start(bf16[2,768,128]{2,1,0:T(8,128)(2,1)S(1)} %pad_maximum_fusion), channel_id=1, source_target_pairs={{0,8},{1,9},{2,10},{3,11},{4,12},{5,13},{6,14},{7,15},{8,16},{9,17... | collective-permute-start | bytes 1179656 | tf_op jit(solution)/shard_map/ppermute | solution.py:256
  8.1 46.1 %collective-permute-start = (bf16[2,256,128]{2,1,0:T(8,128)(2,1)S(1)}, bf16[2,256,128]{2,1,0:T(8,128)(2,1)S(1)}, u32[]{:S(2)}, u32[]{:S(2)}) collective-permute-start(bf16[2,256,128]{2,1,0:T(8,128)(2,1)S(1)} %pad_maximum_fusion.1), channel_id=1, source_target_pairs={{0,8},{1,9},{2,10},{3,11},{4,12},{5,13},{6,14},{7,15},{8,16},{9,17... | collective-permute-start | bytes 393224 | tf_op jit(solution)/shard_map/ppermute | solution.py:257
  46.7 0.7 %copy-start = (bf16[2,768,128]{2,1,0:T(8,128)(2,1)}, bf16[2,768,128]{2,1,0:T(8,128)(2,1)S(1)}, u32[]{:S(2)}) copy-start(bf16[2,768,128]{2,1,0:T(8,128)(2,1)S(1)} %collective-permute-done.1.chunk_ref) | copy-start | bytes 1179652
  54.2 0.7 %copy-start.1 = (bf16[2,256,128]{2,1,0:T(8,128)(2,1)}, bf16[2,256,128]{2,1,0:T(8,128)(2,1)S(1)}, u32[]{:S(2)}) copy-start(bf16[2,256,128]{2,1,0:T(8,128)(2,1)S(1)} %collective-permute-done.chunk_ref) | copy-start | bytes 393220

commit v4 on v2

--- a/solution.py
+++ b/solution.py
@@ -9,6 +9,7 @@
 QPK = 2
 WINDOW = 1024
 QUERY_TILE = 256
+HALO_TILE = 128
 LANES = 128
 
 
@@ -53,22 +54,22 @@
             out_ref[first_row:high_key, :] = (context / row_total).astype(out_ref.dtype)
 
 
-def halo_tile(first_row, shut, q_ref, halo_ref, stats_ref, acc_ref, out_ref):
-    window = halo_ref.shape[1]
-    query_tile = q_ref[...]
-    near_row = first_row + QUERY_TILE
-    near = tile_scores(query_tile, halo_ref[0, first_row:near_row, :])
-    above = lax.broadcasted_iota(jnp.int32, near.shape, 1) > lax.broadcasted_iota(
-        jnp.int32, near.shape, 0
-    )
-    near = jnp.where(above, near, -jnp.inf)
-    parts = [(near, halo_ref[1, first_row:near_row, :])]
-    if near_row < window:
-        far = tile_scores(query_tile, halo_ref[0, near_row:window, :])
-        parts.append((far, halo_ref[1, near_row:window, :]))
-    local_top = stats_ref[:, 0:1]
-    local_total = stats_ref[:, LANES // 2 : LANES // 2 + 1]
-    local_context = acc_ref[...]
+def merge_tile(query_tile, key_ref, value_ref, first_row, low_key, high_key, local):
+    parts = []
+    far_key = low_key
+    if first_row >= low_key:
+        near_row = first_row + query_tile.shape[0]
+        near = tile_scores(query_tile, key_ref[first_row:near_row, :])
+        above = lax.broadcasted_iota(jnp.int32, near.shape, 1) > lax.broadcasted_iota(
+            jnp.int32, near.shape, 0
+        )
+        near = jnp.where(above, near, -jnp.inf)
+        parts.append((near, value_ref[first_row:near_row, :]))
+        far_key = near_row
+    if far_key < high_key:
+        far = tile_scores(query_tile, key_ref[far_key:high_key, :])
+        parts.append((far, value_ref[far_key:high_key, :]))
+    local_top, local_total, local_context = local
     row_top = local_top
     for scores, _ in parts:
         row_top = jnp.maximum(row_top, jnp.max(scores, axis=1, keepdims=True))
@@ -81,19 +82,36 @@
         context = context + jnp.dot(
             probable.astype(jnp.bfloat16), values, preferred_element_type=jnp.float32
         )
-    joined = context / row_total
-    alone = local_context / local_total
-    out_ref[...] = jnp.where(shut, alone, joined).astype(out_ref.dtype)
-
-
-def halo_kernel(opening_ref, q_ref, halo_ref, stats_ref, acc_ref, _, out_ref):
-    tile = pl.program_id(1)
+    return row_top, row_total, context
+
+
+def read_stats(stats_ref, acc_ref, first_row, rows):
+    high_row = first_row + rows
+    return (
+        stats_ref[first_row:high_row, 0:1],
+        stats_ref[first_row:high_row, LANES // 2 : LANES // 2 + 1],
+        acc_ref[first_row:high_row, :],
+    )
+
+
+def finish(shut, local, merged):
+    joined = merged[2] / merged[1]
+    alone = local[2] / local[1]
+    return jnp.where(shut, alone, joined)
+
+
+def halo_kernel(opening_ref, q_ref, key_ref, value_ref, stats_ref, acc_ref, partial_ref, out_ref):
+    halo_rows = stats_ref.shape[0]
     shut = opening_ref[0] != 0
-    for index in range(pl.num_programs(1)):
-
-        @pl.when(tile == index)
-        def _():
-            halo_tile(index * QUERY_TILE, shut, q_ref, halo_ref, stats_ref, acc_ref, out_ref)
+    out_ref[halo_rows:, :] = partial_ref[halo_rows:, :]
+    for first_row in range(0, halo_rows, HALO_TILE):
+        high_row = first_row + HALO_TILE
+        local = read_stats(stats_ref, acc_ref, first_row, HALO_TILE)
+        merged = merge_tile(
+            q_ref[first_row:high_row, :], key_ref, value_ref, first_row, first_row, halo_rows,
+            local,
+        )
+        out_ref[first_row:high_row, :] = finish(shut, local, merged).astype(out_ref.dtype)
 
 
 def local_part(query_local, key_local, value_local, halo_rows):
@@ -123,39 +141,32 @@
     )(query_local, key_local, value_local)
 
 
-def halo_part(opening, query_local, halo, stats, acc, partial_out):
+def halo_part(opening, query_local, halo_keys, halo_values, stats, acc, partial_out):
     row_count, width = query_local.shape
-    head_size = halo.shape[2]
-    window = halo.shape[1]
+    window, head_size = halo_keys.shape
     heads = width // head_size
     halo_rows = stats.shape[1]
-    tiles = halo_rows // QUERY_TILE
-    query_block = pl.BlockSpec((QUERY_TILE, head_size), lambda p, i, o: (i, p))
-    stat_block = pl.BlockSpec((None, QUERY_TILE, LANES), lambda p, i, o: (p, i, 0))
-    acc_block = pl.BlockSpec((None, QUERY_TILE, head_size), lambda p, i, o: (p, i, 0))
+    column = pl.BlockSpec((row_count, head_size), lambda p, o: (0, p))
+    halo_block = pl.BlockSpec((window, head_size), lambda p, o: (0, 0))
+    stat_block = pl.BlockSpec((None, halo_rows, LANES), lambda p, o: (p, 0, 0))
+    acc_block = pl.BlockSpec((None, halo_rows, head_size), lambda p, o: (p, 0, 0))
     flops = 2 * heads * halo_rows * window * head_size
     return pl.pallas_call(
         halo_kernel,
         grid_spec=pltpu.PrefetchScalarGridSpec(
             num_scalar_prefetch=1,
-            grid=(heads, tiles),
-            in_specs=[
-                query_block,
-                pl.BlockSpec(memory_space=pltpu.VMEM),
-                stat_block,
-                acc_block,
-                pl.BlockSpec(memory_space=pl.ANY),
-            ],
-            out_specs=query_block,
+            grid=(heads,),
+            in_specs=[column, halo_block, halo_block, stat_block, acc_block, column],
+            out_specs=column,
         ),
         out_shape=jax.ShapeDtypeStruct((row_count, width), partial_out.dtype),
-        input_output_aliases={5: 0},
+        input_output_aliases={6: 0},
         cost_estimate=pl.CostEstimate(
             flops=flops,
             transcendentals=heads * halo_rows * window // 2,
-            bytes_accessed=2 * halo_rows * width * 2 + 8 * heads * halo_rows * LANES,
+            bytes_accessed=3 * row_count * width * 2 + 8 * heads * halo_rows * LANES,
         ),
-    )(opening, query_local, halo, stats, acc, partial_out)
+    )(opening, query_local, halo_keys, halo_values, stats, acc, partial_out)
 
 
 def per_device(queries, key_rows, value_rows):
@@ -169,7 +180,6 @@
     query_local = queries[0, 0]
     key_local = key_rows[0, 0]
     value_local = value_rows[0, 0]
-    halo_source = jnp.stack([key_local[row_count - WINDOW :], value_local[row_count - WINDOW :]])
     route = []
     for s in range(seq_count):
         for m in range(model_count):
@@ -177,10 +187,11 @@
                 route.append((s * model_count + m - KVH, s * model_count + m))
             elif s > 0:
                 route.append(((s - 1) * model_count + (blocks - 1) * KVH + m, s * model_count + m))
-    halo = lax.ppermute(halo_source, ("seq", "mp"), route)
-    halo_rows = -(-(WINDOW - 1) // QUERY_TILE) * QUERY_TILE
+    halo_keys = lax.ppermute(key_local[row_count - WINDOW :], ("seq", "mp"), route)
+    halo_values = lax.ppermute(value_local[row_count - WINDOW :], ("seq", "mp"), route)
+    halo_rows = WINDOW
     partial_out, stats, acc = local_part(query_local, key_local, value_local, halo_rows)
-    attended = halo_part(opening, query_local, halo, stats, acc, partial_out)
+    attended = halo_part(opening, query_local, halo_keys, halo_values, stats, acc, partial_out)
     return attended.reshape(1, 1, row_count, queries.shape[3])
 
 

time: 58.8 us -> 56.4 us (0.959)
  waiting for transfers between devices: 34.8 us -> 25.2 us
  starting transfers between devices: 6.09 us -> 13.4 us
    ppermute x1 -> x2, waiting for transfers between devices: 34.8 us -> 25.2 us  [the longest x1 13.1 us: per_device(): lax.ppermute(key_local[row_count - WINDOW:], ('seq', 'mp'), route)]
    ppermute x1 -> x2, starting transfers between devices: 6.09 us -> 13.4 us  [the longest x1 7.3 us: per_device(): lax.ppermute(key_local[row_count - WINDOW:], ('seq', 'mp'), route)]
    another operation x1 -> x0, local copies, waits for them, and re-layouts: 1.06 us -> none  [per_device(): jnp.stack([key_local[row_count - WINDOW:], value_local[row_count - WINDOW...]
    slice x0 -> x2, local copies, waits for them, and re-layouts: none -> 1.03 us  [the longest x1 1.01 us: per_device(): value_local[row_count - WINDOW:]]
  transfers between devices with their start and end apart: 1 -> 2, of which waited for: 1 -> 2; matrix products, arithmetic and copies ran while one was open for 0% -> 0% of each run, Pallas kernels for 12% -> 13%
where the time goes in v4:
time: 56.4 us; the launch traced here: 56.2 us
  waiting for transfers between devices  25.2 us (45%)
  Pallas kernels  15.8 us (28%)
  starting transfers between devices  13.4 us (24%)
  local copies, waits for them, and re-layouts  1.74 us (3%)
    ppermute x1, waiting for transfers between devices, per_device(): lax.ppermute(key_local[row_count - WINDOW:], ('seq', 'mp'), route)  13.1 us
    ppermute x1, waiting for transfers between devices, per_device(): lax.ppermute(value_local[row_count - WINDOW:], ('seq', 'mp'), route)  12.1 us
    pallas_call x1, Pallas kernels, halo_part(): pl.pallas_call(halo_kernel, grid_spec=pltpu.PrefetchScalarGridSpec(num_sc...  8.75 us
    ppermute x1, starting transfers between devices, per_device(): lax.ppermute(key_local[row_count - WINDOW:], ('seq', 'mp'), route)  7.3 us
    pallas_call x1, Pallas kernels, local_part(): pl.pallas_call(local_kernel, grid=(heads,), in_specs=[head_block, whole,...  7.04 us
    ppermute x1, starting transfers between devices, per_device(): lax.ppermute(value_local[row_count - WINDOW:], ('seq', 'mp'), route)  6.09 us
  transfers between devices with their start and end apart: 2, of which 2 were waited for; matrix products, arithmetic and copies ran while one was open for 0% of the time, Pallas kernels for 13%

profile of v4, /device:TPU:6, one launch (start us, length us, event | category | flops | bytes accessed | tf_op | source)
XLA Modules:
  0.0 56.2 jit_solution(1855075488085107729)
XLA Ops:
  0.0 0.0 copy-start.2
  0.0 1.0 %slice_bitcast_fusion = bf16[1024,128]{1,0:T(8,128)(2,1)S(1)} fusion(bf16[1,1,1280,128]{3,2,1,0:T(8,128)(2,1)} %param.5), kind=kLoop, calls=%fused_computation | loop fusion | bytes 524288 | tf_op jit(solution)/shard_map/slice | solution.py:191
  1.0 6.1 %collective-permute-start.1 = (bf16[1024,128]{1,0:T(8,128)(2,1)S(1)}, bf16[1024,128]{1,0:T(8,128)(2,1)S(1)}, u32[]{:S(2)}, u32[]{:S(2)}) collective-permute-start(bf16[1024,128]{1,0:T(8,128)(2,1)S(1)} %slice_bitcast_fusion), channel_id=1, source_target_pairs={{0,8},{1,9},{2,10},{3,11},{4,12},{5,13},{6,14},{7,15},{8,16},{9,17... | collective-permute-start | bytes 786440 | tf_op jit(solution)/shard_map/ppermute | solution.py:191
  7.1 0.0 copy-done.2
  7.2 7.3 %collective-permute-start = (bf16[1024,128]{1,0:T(8,128)(2,1)S(1)}, bf16[1024,128]{1,0:T(8,128)(2,1)S(1)}, u32[]{:S(2)}, u32[]{:S(2)}) collective-permute-start(bf16[1024,128]{1,0:T(8,128)(2,1)S(1)} %slice_bitcast_fusion.1), channel_id=1, source_target_pairs={{0,8},{1,9},{2,10},{3,11},{4,12},{5,13},{6,14},{7,15},{8,16},{9,17... | collective-permute-start | bytes 786440 | tf_op jit(solution)/shard_map/ppermute | solution.py:190
  14.5 7.0 %shard_map.37 = (bf16[1280,256]{1,0:T(8,128)(2,1)}, f32[2,1024,128]{2,1,0:T(8,128)}, f32[2,1024,128]{2,1,0:T(8,128)}) custom-call(bf16[1280,256]{1,0:T(8,128)(2,1)} %bitcast.9, bf16[1280,128]{1,0:T(8,128)(2,1)} %bitcast.11, bf16[1280,128]{1,0:T(8,128)(2,1)} %bitcast.12), custom_call_target="tpu_custom_call" | custom-call | flops 1677721600 | bytes 3407872 | tf_op jit(solution)/shard_map/pallas_call | solution.py:126
  21.5 12.1 %collective-permute-done.1.value_ref = bf16[1024,128]{1,0:T(8,128)(2,1)S(1)} collective-permute-done((bf16[1024,128]{1,0:T(8,128)(2,1)S(1)}, bf16[1024,128]{1,0:T(8,128)(2,1)S(1)}, u32[]{:S(2)}, u32[]{:S(2)}) %collective-permute-start.1) | collective-permute-done | bytes 262176 | tf_op jit(solution)/shard_map/ppermute | solution.py:191
  33.6 0.0 copy-start
  33.6 13.1 %collective-permute-done.key_ref = bf16[1024,128]{1,0:T(8,128)(2,1)S(1)} collective-permute-done((bf16[1024,128]{1,0:T(8,128)(2,1)S(1)}, bf16[1024,128]{1,0:T(8,128)(2,1)S(1)}, u32[]{:S(2)}, u32[]{:S(2)}) %collective-permute-start) | collective-permute-done | bytes 262176 | tf_op jit(solution)/shard_map/ppermute | solution.py:190
  46.7 0.0 copy-start.1
  46.7 0.0 copy-done
  46.7 0.7 %copy-done.1 = bf16[1024,128]{1,0:T(8,128)(2,1)} copy-done((bf16[1024,128]{1,0:T(8,128)(2,1)}, bf16[1024,128]{1,0:T(8,128)(2,1)S(1)}, u32[]{:S(2)}) %copy-start.1) | copy-done | bytes 262168
  47.4 8.8 %shard_map.38 = bf16[1280,256]{1,0:T(8,128)(2,1)} custom-call(s32[1]{0:T(128)} %bitcast.opening_ref, bf16[1280,256]{1,0:T(8,128)(2,1)} %bitcast.10, bf16[1024,128]{1,0:T(8,128)(2,1)} %copy-done.1, bf16[1024,128]{1,0:T(8,128)(2,1)} %copy-done, f32[2,1024,128]{2,1,0:T(8,128)} %get-tuple-element.8.stats_ref, ...), custom_call_target="tpu_custom_call", output_to_operand_aliasing={{}: (6, {})} | custom-call | flops 536870912 | bytes 4063232 | tf_op jit(solution)/shard_map/pallas_call | solution.py:154
  (1 shorter events, 0.0 us)
Async XLA Ops:
  0.0 7.1 %copy-start.2 = (bf16[1,1,1280,128]{3,2,1,0:T(8,128)(2,1)S(1)}, bf16[1,1,1280,128]{3,2,1,0:T(8,128)(2,1)}, u32[]{:S(2)}) copy-start(bf16[1,1,1280,128]{3,2,1,0:T(8,128)(2,1)} %param.4) | copy-start | bytes 983044
  1.0 32.6 %collective-permute-start.1 = (bf16[1024,128]{1,0:T(8,128)(2,1)S(1)}, bf16[1024,128]{1,0:T(8,128)(2,1)S(1)}, u32[]{:S(2)}, u32[]{:S(2)}) collective-permute-start(bf16[1024,128]{1,0:T(8,128)(2,1)S(1)} %slice_bitcast_fusion), channel_id=1, source_target_pairs={{0,8},{1,9},{2,10},{3,11},{4,12},{5,13},{6,14},{7,15},{8,16},{9,17... | collective-permute-start | bytes 786440 | tf_op jit(solution)/shard_map/ppermute | solution.py:191
  7.2 39.6 %collective-permute-start = (bf16[1024,128]{1,0:T(8,128)(2,1)S(1)}, bf16[1024,128]{1,0:T(8,128)(2,1)S(1)}, u32[]{:S(2)}, u32[]{:S(2)}) collective-permute-start(bf16[1024,128]{1,0:T(8,128)(2,1)S(1)} %slice_bitcast_fusion.1), channel_id=1, source_target_pairs={{0,8},{1,9},{2,10},{3,11},{4,12},{5,13},{6,14},{7,15},{8,16},{9,17... | collective-permute-start | bytes 786440 | tf_op jit(solution)/shard_map/ppermute | solution.py:190
  33.6 13.1 %copy-start = (bf16[1024,128]{1,0:T(8,128)(2,1)}, bf16[1024,128]{1,0:T(8,128)(2,1)S(1)}, u32[]{:S(2)}) copy-start(bf16[1024,128]{1,0:T(8,128)(2,1)S(1)} %collective-permute-done.1.value_ref) | copy-start | bytes 786436
  46.7 0.7 %copy-start.1 = (bf16[1024,128]{1,0:T(8,128)(2,1)}, bf16[1024,128]{1,0:T(8,128)(2,1)S(1)}, u32[]{:S(2)}) copy-start(bf16[1024,128]{1,0:T(8,128)(2,1)S(1)} %collective-permute-done.key_ref) | copy-start | bytes 786436

commit v5 on v4

--- a/solution.py
+++ b/solution.py
@@ -9,7 +9,6 @@
 QPK = 2
 WINDOW = 1024
 QUERY_TILE = 256
-HALO_TILE = 128
 LANES = 128
 
 
@@ -54,37 +53,6 @@
             out_ref[first_row:high_key, :] = (context / row_total).astype(out_ref.dtype)
 
 
-def merge_tile(query_tile, key_ref, value_ref, first_row, low_key, high_key, local):
-    parts = []
-    far_key = low_key
-    if first_row >= low_key:
-        near_row = first_row + query_tile.shape[0]
-        near = tile_scores(query_tile, key_ref[first_row:near_row, :])
-        above = lax.broadcasted_iota(jnp.int32, near.shape, 1) > lax.broadcasted_iota(
-            jnp.int32, near.shape, 0
-        )
-        near = jnp.where(above, near, -jnp.inf)
-        parts.append((near, value_ref[first_row:near_row, :]))
-        far_key = near_row
-    if far_key < high_key:
-        far = tile_scores(query_tile, key_ref[far_key:high_key, :])
-        parts.append((far, value_ref[far_key:high_key, :]))
-    local_top, local_total, local_context = local
-    row_top = local_top
-    for scores, _ in parts:
-        row_top = jnp.maximum(row_top, jnp.max(scores, axis=1, keepdims=True))
-    rescale = jnp.exp(local_top - row_top)
-    context = rescale * local_context
-    row_total = rescale * local_total
-    for scores, values in parts:
-        probable = jnp.exp(scores - row_top)
-        row_total = row_total + jnp.sum(probable, axis=1, keepdims=True)
-        context = context + jnp.dot(
-            probable.astype(jnp.bfloat16), values, preferred_element_type=jnp.float32
-        )
-    return row_top, row_total, context
-
-
 def read_stats(stats_ref, acc_ref, first_row, rows):
     high_row = first_row + rows
     return (
@@ -94,24 +62,56 @@
     )
 
 
-def finish(shut, local, merged):
-    joined = merged[2] / merged[1]
-    alone = local[2] / local[1]
-    return jnp.where(shut, alone, joined)
-
-
-def halo_kernel(opening_ref, q_ref, key_ref, value_ref, stats_ref, acc_ref, partial_ref, out_ref):
+def weigh_kernel(opening_ref, q_ref, key_ref, stats_ref, weight_ref, merged_ref):
     halo_rows = stats_ref.shape[0]
+    window = key_ref.shape[0]
+    shut = opening_ref[0] != 0
+    column = 0
+    for first_row in range(0, halo_rows, QUERY_TILE):
+        high_row = first_row + QUERY_TILE
+        local_top, local_total, _ = read_stats(stats_ref, stats_ref, first_row, QUERY_TILE)
+        query_tile = q_ref[first_row:high_row, :]
+        near = tile_scores(query_tile, key_ref[first_row:high_row, :])
+        above = lax.broadcasted_iota(jnp.int32, near.shape, 1) > lax.broadcasted_iota(
+            jnp.int32, near.shape, 0
+        )
+        parts = [jnp.where(above, near, -jnp.inf)]
+        if high_row < window:
+            parts.append(tile_scores(query_tile, key_ref[high_row:window, :]))
+        row_top = local_top
+        for scores in parts:
+            row_top = jnp.maximum(row_top, jnp.max(scores, axis=1, keepdims=True))
+        rescale = jnp.exp(local_top - row_top)
+        row_total = rescale * local_total
+        for scores in parts:
+            probable = jnp.exp(scores - row_top)
+            row_total = row_total + jnp.sum(probable, axis=1, keepdims=True)
+            width = scores.shape[1]
+            weight_ref[:, column : column + width] = probable.astype(weight_ref.dtype)
+            column += width
+        rescale = jnp.where(shut, 1.0, rescale)
+        row_total = jnp.where(shut, local_total, row_total)
+        merged_ref[first_row:high_row, :] = packed_stats(rescale, row_total)
+
+
+def gather_kernel(opening_ref, weight_ref, value_ref, merged_ref, acc_ref, partial_ref, out_ref):
+    halo_rows = merged_ref.shape[0]
+    window = value_ref.shape[0]
     shut = opening_ref[0] != 0
     out_ref[halo_rows:, :] = partial_ref[halo_rows:, :]
-    for first_row in range(0, halo_rows, HALO_TILE):
-        high_row = first_row + HALO_TILE
-        local = read_stats(stats_ref, acc_ref, first_row, HALO_TILE)
-        merged = merge_tile(
-            q_ref[first_row:high_row, :], key_ref, value_ref, first_row, first_row, halo_rows,
-            local,
+    column = 0
+    for first_row in range(0, halo_rows, QUERY_TILE):
+        high_row = first_row + QUERY_TILE
+        rescale, row_total, local_context = read_stats(merged_ref, acc_ref, first_row, QUERY_TILE)
+        width = window - first_row
+        context = jnp.dot(
+            weight_ref[:, column : column + width],
+            value_ref[first_row:window, :],
+            preferred_element_type=jnp.float32,
         )
-        out_ref[first_row:high_row, :] = finish(shut, local, merged).astype(out_ref.dtype)
+        column += width
+        context = rescale * local_context + jnp.where(shut, 0.0, context)
+        out_ref[first_row:high_row, :] = (context / row_total).astype(out_ref.dtype)
 
 
 def local_part(query_local, key_local, value_local, halo_rows):
@@ -141,32 +141,69 @@
     )(query_local, key_local, value_local)
 
 
-def halo_part(opening, query_local, halo_keys, halo_values, stats, acc, partial_out):
+def packed_width(halo_rows, window):
+    return sum(window - first_row for first_row in range(0, halo_rows, QUERY_TILE))
+
+
+def weigh_part(opening, query_local, halo_keys, stats):
     row_count, width = query_local.shape
     window, head_size = halo_keys.shape
     heads = width // head_size
     halo_rows = stats.shape[1]
+    weight_width = packed_width(halo_rows, window)
+    column = pl.BlockSpec((row_count, head_size), lambda p, o: (0, p))
+    halo_block = pl.BlockSpec((window, head_size), lambda p, o: (0, 0))
+    stat_block = pl.BlockSpec((None, halo_rows, LANES), lambda p, o: (p, 0, 0))
+    weight_block = pl.BlockSpec((None, QUERY_TILE, weight_width), lambda p, o: (p, 0, 0))
+    return pl.pallas_call(
+        weigh_kernel,
+        grid_spec=pltpu.PrefetchScalarGridSpec(
+            num_scalar_prefetch=1,
+            grid=(heads,),
+            in_specs=[column, halo_block, stat_block],
+            out_specs=[weight_block, stat_block],
+        ),
+        out_shape=[
+            jax.ShapeDtypeStruct((heads, QUERY_TILE, weight_width), jnp.bfloat16),
+            jax.ShapeDtypeStruct((heads, halo_rows, LANES), jnp.float32),
+        ],
+        cost_estimate=pl.CostEstimate(
+            flops=2 * heads * QUERY_TILE * weight_width * head_size,
+            transcendentals=heads * QUERY_TILE * weight_width,
+            bytes_accessed=row_count * width * 2 + 2 * heads * QUERY_TILE * weight_width
+            + 8 * heads * halo_rows * LANES,
+        ),
+    )(opening, query_local, halo_keys, stats)
+
+
+def gather_part(opening, weights, halo_values, merged, acc, partial_out):
+    row_count, width = partial_out.shape
+    window, head_size = halo_values.shape
+    heads = width // head_size
+    halo_rows = merged.shape[1]
+    weight_width = weights.shape[2]
     column = pl.BlockSpec((row_count, head_size), lambda p, o: (0, p))
     halo_block = pl.BlockSpec((window, head_size), lambda p, o: (0, 0))
     stat_block = pl.BlockSpec((None, halo_rows, LANES), lambda p, o: (p, 0, 0))
     acc_block = pl.BlockSpec((None, halo_rows, head_size), lambda p, o: (p, 0, 0))
-    flops = 2 * heads * halo_rows * window * head_size
+    weight_block = pl.BlockSpec((None, QUERY_TILE, weight_width), lambda p, o: (p, 0, 0))
     return pl.pallas_call(
-        halo_kernel,
+        gather_kernel,
         grid_spec=pltpu.PrefetchScalarGridSpec(
             num_scalar_prefetch=1,
             grid=(heads,),
-            in_specs=[column, halo_block, halo_block, stat_block, acc_block, column],
+            in_specs=[weight_block, halo_block, stat_block, acc_block, column],
             out_specs=column,
         ),
         out_shape=jax.ShapeDtypeStruct((row_count, width), partial_out.dtype),
-        input_output_aliases={6: 0},
+        input_output_aliases={5: 0},
         cost_estimate=pl.CostEstimate(
-            flops=flops,
-            transcendentals=heads * halo_rows * window // 2,
-            bytes_accessed=3 * row_count * width * 2 + 8 * heads * halo_rows * LANES,
-        ),
-    )(opening, query_local, halo_keys, halo_values, stats, acc, partial_out)
+            flops=2 * heads * QUERY_TILE * weight_width * head_size,
+            transcendentals=0,
+            bytes_accessed=2 * heads * QUERY_TILE * weight_width + 2 * row_count * width * 2
+            + 8 * heads * halo_rows * LANES,
+        ),
+    )(opening, weights, halo_values, merged, acc, partial_out)
 
 
 def per_device(queries, key_rows, value_rows):
@@ -191,7 +228,8 @@
     halo_values = lax.ppermute(value_local[row_count - WINDOW :], ("seq", "mp"), route)
     halo_rows = WINDOW
     partial_out, stats, acc = local_part(query_local, key_local, value_local, halo_rows)
-    attended = halo_part(opening, query_local, halo_keys, halo_values, stats, acc, partial_out)
+    weights, merged = weigh_part(opening, query_local, halo_keys, stats)
+    attended = gather_part(opening, weights, halo_values, merged, acc, partial_out)
     return attended.reshape(1, 1, row_count, queries.shape[3])
 
 

time: 56.4 us -> 50 us (0.89)
  waiting for transfers between devices: 25.2 us -> 14.4 us
  Pallas kernels: 15.8 us -> 18.6 us
  local copies, waits for them, and re-layouts: 1.74 us -> 3.35 us
    ppermute x1, waiting for transfers between devices: 12.1 us -> 3.18 us  [per_device(): lax.ppermute(value_local[row_count - WINDOW:], ('seq', 'mp'), route)]
    pallas_call x1 -> x2, Pallas kernels: 8.75 us -> 11.5 us  [the longest x1 7.74 us: weigh_part(): pl.pallas_call(weigh_kernel, grid_spec=pltpu.PrefetchScalarGridSpec(num_s...]
    ppermute x1, waiting for transfers between devices: 13.1 us -> 11.2 us  [per_device(): lax.ppermute(key_local[row_count - WINDOW:], ('seq', 'mp'), route)]
    ppermute x1, starting transfers between devices: 6.09 us -> 7.3 us  [per_device(): lax.ppermute(value_local[row_count - WINDOW:], ('seq', 'mp'), route)]
    ppermute x1, starting transfers between devices: 7.3 us -> 6.09 us  [per_device(): lax.ppermute(key_local[row_count - WINDOW:], ('seq', 'mp'), route)]
    slice x1, local copies, waits for them, and re-layouts: 0.02 us -> 0.97 us  [per_device(): key_local[row_count - WINDOW:]]
    unnamed x6 -> x4, local copies, waits for them, and re-layouts: 0.71 us -> 1.41 us
  transfers between devices with their start and end apart: 2 -> 2, of which waited for: 2 -> 2; matrix products, arithmetic and copies ran while one was open for 0% -> 2% of each run, Pallas kernels for 13% -> 30%
where the time goes in v5:
time: 50 us; the launch traced here: 49.8 us
  Pallas kernels  18.6 us (37%)
  waiting for transfers between devices  14.4 us (29%)
  starting transfers between devices  13.4 us (27%)
  local copies, waits for them, and re-layouts  3.35 us (7%)
    ppermute x1, waiting for transfers between devices, per_device(): lax.ppermute(key_local[row_count - WINDOW:], ('seq', 'mp'), route)  11.2 us
    pallas_call x1, Pallas kernels, weigh_part(): pl.pallas_call(weigh_kernel, grid_spec=pltpu.PrefetchScalarGridSpec(num_s...  7.74 us
    ppermute x1, starting transfers between devices, per_device(): lax.ppermute(value_local[row_count - WINDOW:], ('seq', 'mp'), route)  7.3 us
    pallas_call x1, Pallas kernels, local_part(): pl.pallas_call(local_kernel, grid=(heads,), in_specs=[head_block, whole,...  7.03 us
    ppermute x1, starting transfers between devices, per_device(): lax.ppermute(key_local[row_count - WINDOW:], ('seq', 'mp'), route)  6.09 us
    pallas_call x1, Pallas kernels, gather_part(): pl.pallas_call(gather_kernel, grid_spec=pltpu.PrefetchScalarGridSpec(num_...  3.8 us
    ppermute x1, waiting for transfers between devices, per_device(): lax.ppermute(value_local[row_count - WINDOW:], ('seq', 'mp'), route)  3.18 us
    unnamed x4, local copies, waits for them, and re-layouts  1.41 us
  transfers between devices with their start and end apart: 2, of which 2 were waited for; matrix products, arithmetic and copies ran while one was open for 2% of the time, Pallas kernels for 30%

profile of v5, /device:TPU:6, one launch (start us, length us, event | category | flops | bytes accessed | tf_op | source)
XLA Modules:
  0.0 49.8 jit_solution(17696732253511196289)
XLA Ops:
  0.0 1.0 %slice_bitcast_fusion.1 = bf16[1024,128]{1,0:T(8,128)(2,1)S(1)} fusion(bf16[1,1,1280,128]{3,2,1,0:T(8,128)(2,1)} %param.4), kind=kLoop, calls=%fused_computation.1 | loop fusion | bytes 524288 | tf_op jit(solution)/shard_map/slice | solution.py:227
  1.0 6.1 %collective-permute-start = (bf16[1024,128]{1,0:T(8,128)(2,1)S(1)}, bf16[1024,128]{1,0:T(8,128)(2,1)S(1)}, u32[]{:S(2)}, u32[]{:S(2)}) collective-permute-start(bf16[1024,128]{1,0:T(8,128)(2,1)S(1)} %slice_bitcast_fusion.1), channel_id=1, source_target_pairs={{0,8},{1,9},{2,10},{3,11},{4,12},{5,13},{6,14},{7,15},{8,16},{9,17... | collective-permute-start | bytes 786440 | tf_op jit(solution)/shard_map/ppermute | solution.py:227
  7.1 1.0 %slice_bitcast_fusion = bf16[1024,128]{1,0:T(8,128)(2,1)S(1)} fusion(bf16[1,1,1280,128]{3,2,1,0:T(8,128)(2,1)} %param.5), kind=kLoop, calls=%fused_computation | loop fusion | bytes 524288 | tf_op jit(solution)/shard_map/slice | solution.py:228
  8.0 7.3 %collective-permute-start.1 = (bf16[1024,128]{1,0:T(8,128)(2,1)S(1)}, bf16[1024,128]{1,0:T(8,128)(2,1)S(1)}, u32[]{:S(2)}, u32[]{:S(2)}) collective-permute-start(bf16[1024,128]{1,0:T(8,128)(2,1)S(1)} %slice_bitcast_fusion), channel_id=1, source_target_pairs={{0,8},{1,9},{2,10},{3,11},{4,12},{5,13},{6,14},{7,15},{8,16},{9,17... | collective-permute-start | bytes 786440 | tf_op jit(solution)/shard_map/ppermute | solution.py:228
  15.4 7.0 %shard_map.37 = (bf16[1280,256]{1,0:T(8,128)(2,1)}, f32[2,1024,128]{2,1,0:T(8,128)}, f32[2,1024,128]{2,1,0:T(8,128)}) custom-call(bf16[1280,256]{1,0:T(8,128)(2,1)} %bitcast.11, bf16[1280,128]{1,0:T(8,128)(2,1)} %bitcast.9, bf16[1280,128]{1,0:T(8,128)(2,1)} %bitcast.10), custom_call_target="tpu_custom_call" | custom-call | flops 1677721600 | bytes 3407872 | tf_op jit(solution)/shard_map/pallas_call | solution.py:126
  22.4 11.2 %collective-permute-done.key_ref = bf16[1024,128]{1,0:T(8,128)(2,1)S(1)} collective-permute-done((bf16[1024,128]{1,0:T(8,128)(2,1)S(1)}, bf16[1024,128]{1,0:T(8,128)(2,1)S(1)}, u32[]{:S(2)}, u32[]{:S(2)}) %collective-permute-start) | collective-permute-done | bytes 262176 | tf_op jit(solution)/shard_map/ppermute | solution.py:227
  33.7 0.0 copy-start.1
  33.7 0.7 %copy-done.1 = bf16[1024,128]{1,0:T(8,128)(2,1)} copy-done((bf16[1024,128]{1,0:T(8,128)(2,1)}, bf16[1024,128]{1,0:T(8,128)(2,1)S(1)}, u32[]{:S(2)}) %copy-start.1) | copy-done | bytes 262168
  34.4 7.7 %shard_map.38 = (bf16[2,256,2560]{2,1,0:T(8,128)(2,1)}, f32[2,1024,128]{2,1,0:T(8,128)}) custom-call(s32[1]{0:T(128)} %bitcast.opening_ref, bf16[1280,256]{1,0:T(8,128)(2,1)} %bitcast.12, bf16[1024,128]{1,0:T(8,128)(2,1)} %copy-done.1, f32[2,1024,128]{2,1,0:T(8,128)} %get-tuple-element.10.stats_ref), custom_call_target="tpu_custom_call" | custom-call | flops 335544320 | bytes 5373952 | tf_op jit(solution)/shard_map/pallas_call | solution.py:158
  42.1 3.2 %collective-permute-done.1.value_ref = bf16[1024,128]{1,0:T(8,128)(2,1)S(1)} collective-permute-done((bf16[1024,128]{1,0:T(8,128)(2,1)S(1)}, bf16[1024,128]{1,0:T(8,128)(2,1)S(1)}, u32[]{:S(2)}, u32[]{:S(2)}) %collective-permute-start.1) | collective-permute-done | bytes 262176 | tf_op jit(solution)/shard_map/ppermute | solution.py:228
  45.3 0.0 copy-start
  45.3 0.7 %copy-done = bf16[1024,128]{1,0:T(8,128)(2,1)} copy-done((bf16[1024,128]{1,0:T(8,128)(2,1)}, bf16[1024,128]{1,0:T(8,128)(2,1)S(1)}, u32[]{:S(2)}) %copy-start) | copy-done | bytes 262168
  46.0 3.8 %shard_map.39 = bf16[1280,256]{1,0:T(8,128)(2,1)} custom-call(s32[1]{0:T(128)} %bitcast.opening_ref, bf16[2,256,2560]{2,1,0:T(8,128)(2,1)} %get-tuple-element.11.weight_ref, bf16[1024,128]{1,0:T(8,128)(2,1)} %copy-done, f32[2,1024,128]{2,1,0:T(8,128)} %get-tuple-element.12.merged_ref, ...), custom_call_target="tpu_custom_call", output_to_operand_aliasing={{}: (5, {})} | custom-call | flops 335544320 | bytes 6029312 | tf_op jit(solution)/shard_map/pallas_call | solution.py:190
Async XLA Ops:
  1.0 32.7 %collective-permute-start = (bf16[1024,128]{1,0:T(8,128)(2,1)S(1)}, bf16[1024,128]{1,0:T(8,128)(2,1)S(1)}, u32[]{:S(2)}, u32[]{:S(2)}) collective-permute-start(bf16[1024,128]{1,0:T(8,128)(2,1)S(1)} %slice_bitcast_fusion.1), channel_id=1, source_target_pairs={{0,8},{1,9},{2,10},{3,11},{4,12},{5,13},{6,14},{7,15},{8,16},{9,17... | collective-permute-start | bytes 786440 | tf_op jit(solution)/shard_map/ppermute | solution.py:227
  8.0 37.2 %collective-permute-start.1 = (bf16[1024,128]{1,0:T(8,128)(2,1)S(1)}, bf16[1024,128]{1,0:T(8,128)(2,1)S(1)}, u32[]{:S(2)}, u32[]{:S(2)}) collective-permute-start(bf16[1024,128]{1,0:T(8,128)(2,1)S(1)} %slice_bitcast_fusion), channel_id=1, source_target_pairs={{0,8},{1,9},{2,10},{3,11},{4,12},{5,13},{6,14},{7,15},{8,16},{9,17... | collective-permute-start | bytes 786440 | tf_op jit(solution)/shard_map/ppermute | solution.py:228
  33.7 0.7 %copy-start.1 = (bf16[1024,128]{1,0:T(8,128)(2,1)}, bf16[1024,128]{1,0:T(8,128)(2,1)S(1)}, u32[]{:S(2)}) copy-start(bf16[1024,128]{1,0:T(8,128)(2,1)S(1)} %collective-permute-done.key_ref) | copy-start | bytes 786436
  45.3 0.7 %copy-start = (bf16[1024,128]{1,0:T(8,128)(2,1)}, bf16[1024,128]{1,0:T(8,128)(2,1)S(1)}, u32[]{:S(2)}) copy-start(bf16[1024,128]{1,0:T(8,128)(2,1)S(1)} %collective-permute-done.1.value_ref) | copy-start | bytes 786436

commit v6 on v5

--- a/solution.py
+++ b/solution.py
@@ -94,11 +94,10 @@
         merged_ref[first_row:high_row, :] = packed_stats(rescale, row_total)
 
 
-def gather_kernel(opening_ref, weight_ref, value_ref, merged_ref, acc_ref, partial_ref, out_ref):
+def gather_kernel(opening_ref, weight_ref, value_ref, merged_ref, acc_ref, _, out_ref):
     halo_rows = merged_ref.shape[0]
     window = value_ref.shape[0]
     shut = opening_ref[0] != 0
-    out_ref[halo_rows:, :] = partial_ref[halo_rows:, :]
     column = 0
     for first_row in range(0, halo_rows, QUERY_TILE):
         high_row = first_row + QUERY_TILE
@@ -182,7 +181,7 @@
     heads = width // head_size
     halo_rows = merged.shape[1]
     weight_width = weights.shape[2]
-    column = pl.BlockSpec((row_count, head_size), lambda p, o: (0, p))
+    column = pl.BlockSpec((halo_rows, head_size), lambda p, o: (0, p))
     halo_block = pl.BlockSpec((window, head_size), lambda p, o: (0, 0))
     stat_block = pl.BlockSpec((None, halo_rows, LANES), lambda p, o: (p, 0, 0))
     acc_block = pl.BlockSpec((None, halo_rows, head_size), lambda p, o: (p, 0, 0))
@@ -192,7 +191,13 @@
         grid_spec=pltpu.PrefetchScalarGridSpec(
             num_scalar_prefetch=1,
             grid=(heads,),
-            in_specs=[weight_block, halo_block, stat_block, acc_block, column],
+            in_specs=[
+                weight_block,
+                halo_block,
+                stat_block,
+                acc_block,
+                pl.BlockSpec(memory_space=pl.ANY),
+            ],
             out_specs=column,
         ),
         out_shape=jax.ShapeDtypeStruct((row_count, width), partial_out.dtype),
@@ -224,8 +229,11 @@
                 route.append((s * model_count + m - KVH, s * model_count + m))
             elif s > 0:
                 route.append(((s - 1) * model_count + (blocks - 1) * KVH + m, s * model_count + m))
-    halo_keys = lax.ppermute(key_local[row_count - WINDOW :], ("seq", "mp"), route)
-    halo_values = lax.ppermute(value_local[row_count - WINDOW :], ("seq", "mp"), route)
+    key_tail, value_tail = lax.optimization_barrier(
+        (key_local[row_count - WINDOW :], value_local[row_count - WINDOW :])
+    )
+    halo_keys = lax.ppermute(key_tail, ("seq", "mp"), route)
+    halo_values = lax.ppermute(value_tail, ("seq", "mp"), route)
     halo_rows = WINDOW
     partial_out, stats, acc = local_part(query_local, key_local, value_local, halo_rows)
     weights, merged = weigh_part(opening, query_local, halo_keys, stats)

time: 50 us -> 51.3 us (1.026)
  waiting for transfers between devices: 14.4 us -> 16.8 us
  local copies, waits for them, and re-layouts: 3.35 us -> 2.49 us
    ppermute x2, waiting for transfers between devices: 14.4 us -> 16.8 us  [the longest x1 12.1 us: per_device(): halo_keys = lax.ppermute(key_tail, ('seq', 'mp'), route)]
    slice x1 -> x0, local copies, waits for them, and re-layouts: 0.97 us -> none  [per_device(): key_local[row_count - WINDOW:]]
  transfers between devices with their start and end apart: 2 -> 2, of which waited for: 2 -> 2; matrix products, arithmetic and copies ran while one was open for 2% -> 0% of each run, Pallas kernels for 30% -> 29%
where the time goes in v6:
time: 51.3 us; the launch traced here: 51.1 us
  Pallas kernels  18.4 us (36%)
  waiting for transfers between devices  16.8 us (33%)
  starting transfers between devices  13.4 us (26%)
  local copies, waits for them, and re-layouts  2.49 us (5%)
    ppermute x1, waiting for transfers between devices, per_device(): halo_keys = lax.ppermute(key_tail, ('seq', 'mp'), route)  12.1 us
    pallas_call x1, Pallas kernels, weigh_part(): pl.pallas_call(weigh_kernel, grid_spec=pltpu.PrefetchScalarGridSpec(num_s...  7.74 us
    ppermute x1, starting transfers between devices, per_device(): halo_values = lax.ppermute(value_tail, ('seq', 'mp'), route)  7.3 us
    pallas_call x1, Pallas kernels, local_part(): pl.pallas_call(local_kernel, grid=(heads,), in_specs=[head_block, whole,...  7.03 us
    ppermute x1, starting transfers between devices, per_device(): halo_keys = lax.ppermute(key_tail, ('seq', 'mp'), route)  6.09 us
    ppermute x1, waiting for transfers between devices, per_device(): halo_values = lax.ppermute(value_tail, ('seq', 'mp'), route)  4.68 us
    pallas_call x1, Pallas kernels, gather_part(): pl.pallas_call(gather_kernel, grid_spec=pltpu.PrefetchScalarGridSpec(num_...  3.59 us
    unnamed x4, local copies, waits for them, and re-layouts  1.43 us
  transfers between devices with their start and end apart: 2, of which 2 were waited for; matrix products, arithmetic and copies ran while one was open for 0% of the time, Pallas kernels for 29%

profile of v6, /device:TPU:6, one launch (start us, length us, event | category | flops | bytes accessed | tf_op | source)
XLA Modules:
  0.0 51.1 jit_solution(5632777791192616172)
XLA Ops:
  0.0 1.1 %slice_bitcast_fusion = (bf16[1024,128]{1,0:T(8,128)(2,1)S(1)}, bf16[1024,128]{1,0:T(8,128)(2,1)S(1)}) fusion(bf16[1,1,1280,128]{3,2,1,0:T(8,128)(2,1)} %param.5, bf16[1,1,1280,128]{3,2,1,0:T(8,128)(2,1)} %param.4), kind=kLoop, calls=%fused_computation | loop fusion | bytes 1048576 | tf_op jit(solution)/shard_map/slice | solution.py:233
  1.1 6.1 %collective-permute-start = (bf16[1024,128]{1,0:T(8,128)(2,1)S(1)}, bf16[1024,128]{1,0:T(8,128)(2,1)S(1)}, u32[]{:S(2)}, u32[]{:S(2)}) collective-permute-start(bf16[1024,128]{1,0:T(8,128)(2,1)S(1)} %get-tuple-element.12), channel_id=1, source_target_pairs={{0,8},{1,9},{2,10},{3,11},{4,12},{5,13},{6,14},{7,15},{8,16},{9,17... | collective-permute-start | bytes 786440 | tf_op jit(solution)/shard_map/ppermute | solution.py:235
  7.2 7.3 %collective-permute-start.1 = (bf16[1024,128]{1,0:T(8,128)(2,1)S(1)}, bf16[1024,128]{1,0:T(8,128)(2,1)S(1)}, u32[]{:S(2)}, u32[]{:S(2)}) collective-permute-start(bf16[1024,128]{1,0:T(8,128)(2,1)S(1)} %get-tuple-element.15), channel_id=1, source_target_pairs={{0,8},{1,9},{2,10},{3,11},{4,12},{5,13},{6,14},{7,15},{8,16},{9,17... | collective-permute-start | bytes 786440 | tf_op jit(solution)/shard_map/ppermute | solution.py:236
  14.5 7.0 %shard_map.37 = (bf16[1280,256]{1,0:T(8,128)(2,1)}, f32[2,1024,128]{2,1,0:T(8,128)}, f32[2,1024,128]{2,1,0:T(8,128)}) custom-call(bf16[1280,256]{1,0:T(8,128)(2,1)} %bitcast.11, bf16[1280,128]{1,0:T(8,128)(2,1)} %bitcast.10, bf16[1280,128]{1,0:T(8,128)(2,1)} %bitcast.9), custom_call_target="tpu_custom_call" | custom-call | flops 1677721600 | bytes 3407872 | tf_op jit(solution)/shard_map/pallas_call | solution.py:125
  21.5 12.1 %collective-permute-done.key_ref = bf16[1024,128]{1,0:T(8,128)(2,1)S(1)} collective-permute-done((bf16[1024,128]{1,0:T(8,128)(2,1)S(1)}, bf16[1024,128]{1,0:T(8,128)(2,1)S(1)}, u32[]{:S(2)}, u32[]{:S(2)}) %collective-permute-start) | collective-permute-done | bytes 262176 | tf_op jit(solution)/shard_map/ppermute | solution.py:235
  33.7 0.0 copy-start.1
  33.7 0.7 %copy-done.1 = bf16[1024,128]{1,0:T(8,128)(2,1)} copy-done((bf16[1024,128]{1,0:T(8,128)(2,1)}, bf16[1024,128]{1,0:T(8,128)(2,1)S(1)}, u32[]{:S(2)}) %copy-start.1) | copy-done | bytes 262168
  34.4 7.7 %shard_map.38 = (bf16[2,256,2560]{2,1,0:T(8,128)(2,1)}, f32[2,1024,128]{2,1,0:T(8,128)}) custom-call(s32[1]{0:T(128)} %bitcast.opening_ref, bf16[1280,256]{1,0:T(8,128)(2,1)} %bitcast.12, bf16[1024,128]{1,0:T(8,128)(2,1)} %copy-done.1, f32[2,1024,128]{2,1,0:T(8,128)} %get-tuple-element.13.stats_ref), custom_call_target="tpu_custom_call" | custom-call | flops 335544320 | bytes 5373952 | tf_op jit(solution)/shard_map/pallas_call | solution.py:157
  42.1 4.7 %collective-permute-done.1.value_ref = bf16[1024,128]{1,0:T(8,128)(2,1)S(1)} collective-permute-done((bf16[1024,128]{1,0:T(8,128)(2,1)S(1)}, bf16[1024,128]{1,0:T(8,128)(2,1)S(1)}, u32[]{:S(2)}, u32[]{:S(2)}) %collective-permute-start.1) | collective-permute-done | bytes 262176 | tf_op jit(solution)/shard_map/ppermute | solution.py:236
  46.8 0.0 copy-start
  46.8 0.7 %copy-done = bf16[1024,128]{1,0:T(8,128)(2,1)} copy-done((bf16[1024,128]{1,0:T(8,128)(2,1)}, bf16[1024,128]{1,0:T(8,128)(2,1)S(1)}, u32[]{:S(2)}) %copy-start) | copy-done | bytes 262168
  47.5 3.6 %shard_map.39 = bf16[1280,256]{1,0:T(8,128)(2,1)} custom-call(s32[1]{0:T(128)} %bitcast.opening_ref, bf16[2,256,2560]{2,1,0:T(8,128)(2,1)} %get-tuple-element.14.weight_ref, bf16[1024,128]{1,0:T(8,128)(2,1)} %copy-done, f32[2,1024,128]{2,1,0:T(8,128)} %get-tuple-element.16.merged_ref, ...), custom_call_target="tpu_custom_call", output_to_operand_aliasing={{}: (5, {})} | custom-call | flops 335544320 | bytes 6029312 | tf_op jit(solution)/shard_map/pallas_call | solution.py:189
Async XLA Ops:
  1.1 32.6 %collective-permute-start = (bf16[1024,128]{1,0:T(8,128)(2,1)S(1)}, bf16[1024,128]{1,0:T(8,128)(2,1)S(1)}, u32[]{:S(2)}, u32[]{:S(2)}) collective-permute-start(bf16[1024,128]{1,0:T(8,128)(2,1)S(1)} %get-tuple-element.12), channel_id=1, source_target_pairs={{0,8},{1,9},{2,10},{3,11},{4,12},{5,13},{6,14},{7,15},{8,16},{9,17... | collective-permute-start | bytes 786440 | tf_op jit(solution)/shard_map/ppermute | solution.py:235
  7.2 39.6 %collective-permute-start.1 = (bf16[1024,128]{1,0:T(8,128)(2,1)S(1)}, bf16[1024,128]{1,0:T(8,128)(2,1)S(1)}, u32[]{:S(2)}, u32[]{:S(2)}) collective-permute-start(bf16[1024,128]{1,0:T(8,128)(2,1)S(1)} %get-tuple-element.15), channel_id=1, source_target_pairs={{0,8},{1,9},{2,10},{3,11},{4,12},{5,13},{6,14},{7,15},{8,16},{9,17... | collective-permute-start | bytes 786440 | tf_op jit(solution)/shard_map/ppermute | solution.py:236
  33.7 0.7 %copy-start.1 = (bf16[1024,128]{1,0:T(8,128)(2,1)}, bf16[1024,128]{1,0:T(8,128)(2,1)S(1)}, u32[]{:S(2)}) copy-start(bf16[1024,128]{1,0:T(8,128)(2,1)S(1)} %collective-permute-done.key_ref) | copy-start | bytes 786436
  46.8 0.7 %copy-start = (bf16[1024,128]{1,0:T(8,128)(2,1)}, bf16[1024,128]{1,0:T(8,128)(2,1)S(1)}, u32[]{:S(2)}) copy-start(bf16[1024,128]{1,0:T(8,128)(2,1)S(1)} %collective-permute-done.1.value_ref) | copy-start | bytes 786436

commit v7 on v6

--- a/solution.py
+++ b/solution.py
@@ -229,11 +229,8 @@
                 route.append((s * model_count + m - KVH, s * model_count + m))
             elif s > 0:
                 route.append(((s - 1) * model_count + (blocks - 1) * KVH + m, s * model_count + m))
-    key_tail, value_tail = lax.optimization_barrier(
-        (key_local[row_count - WINDOW :], value_local[row_count - WINDOW :])
-    )
-    halo_keys = lax.ppermute(key_tail, ("seq", "mp"), route)
-    halo_values = lax.ppermute(value_tail, ("seq", "mp"), route)
+    halo_keys = lax.ppermute(key_local[row_count - WINDOW :], ("seq", "mp"), route)
+    halo_values = lax.ppermute(value_local[row_count - WINDOW :], ("seq", "mp"), route)
     halo_rows = WINDOW
     partial_out, stats, acc = local_part(query_local, key_local, value_local, halo_rows)
     weights, merged = weigh_part(opening, query_local, halo_keys, stats)

time: 51.3 us -> 49.8 us (0.971)
  waiting for transfers between devices: 16.8 us -> 14.4 us
  local copies, waits for them, and re-layouts: 2.49 us -> 3.35 us
    ppermute x2, waiting for transfers between devices: 16.8 us -> 14.4 us  [the longest x1 11.2 us: per_device(): lax.ppermute(key_local[row_count - WINDOW:], ('seq', 'mp'), route)]
    slice x0 -> x1, local copies, waits for them, and re-layouts: none -> 0.97 us  [per_device(): key_local[row_count - WINDOW:]]
  transfers between devices with their start and end apart: 2 -> 2, of which waited for: 2 -> 2; matrix products, arithmetic and copies ran while one was open for 0% -> 2% of each run, Pallas kernels for 29% -> 30%
where the time goes in v7:
time: 49.8 us; the launch traced here: 49.6 us
  Pallas kernels  18.4 us (37%)
  waiting for transfers between devices  14.4 us (29%)
  starting transfers between devices  13.4 us (27%)
  local copies, waits for them, and re-layouts  3.35 us (7%)
    ppermute x1, waiting for transfers between devices, per_device(): lax.ppermute(key_local[row_count - WINDOW:], ('seq', 'mp'), route)  11.2 us
    pallas_call x1, Pallas kernels, weigh_part(): pl.pallas_call(weigh_kernel, grid_spec=pltpu.PrefetchScalarGridSpec(num_s...  7.74 us
    ppermute x1, starting transfers between devices, per_device(): lax.ppermute(value_local[row_count - WINDOW:], ('seq', 'mp'), route)  7.3 us
    pallas_call x1, Pallas kernels, local_part(): pl.pallas_call(local_kernel, grid=(heads,), in_specs=[head_block, whole,...  7.03 us
    ppermute x1, starting transfers between devices, per_device(): lax.ppermute(key_local[row_count - WINDOW:], ('seq', 'mp'), route)  6.09 us
    pallas_call x1, Pallas kernels, gather_part(): pl.pallas_call(gather_kernel, grid_spec=pltpu.PrefetchScalarGridSpec(num_...  3.59 us
    ppermute x1, waiting for transfers between devices, per_device(): lax.ppermute(value_local[row_count - WINDOW:], ('seq', 'mp'), route)  3.18 us
    unnamed x4, local copies, waits for them, and re-layouts  1.41 us
  transfers between devices with their start and end apart: 2, of which 2 were waited for; matrix products, arithmetic and copies ran while one was open for 2% of the time, Pallas kernels for 30%

profile of v7, /device:TPU:6, one launch (start us, length us, event | category | flops | bytes accessed | tf_op | source)
XLA Modules:
  0.0 49.6 jit_solution(4581465383154826178)
XLA Ops:
  0.0 1.0 %slice_bitcast_fusion.1 = bf16[1024,128]{1,0:T(8,128)(2,1)S(1)} fusion(bf16[1,1,1280,128]{3,2,1,0:T(8,128)(2,1)} %param.4), kind=kLoop, calls=%fused_computation.1 | loop fusion | bytes 524288 | tf_op jit(solution)/shard_map/slice | solution.py:232
  1.0 6.1 %collective-permute-start = (bf16[1024,128]{1,0:T(8,128)(2,1)S(1)}, bf16[1024,128]{1,0:T(8,128)(2,1)S(1)}, u32[]{:S(2)}, u32[]{:S(2)}) collective-permute-start(bf16[1024,128]{1,0:T(8,128)(2,1)S(1)} %slice_bitcast_fusion.1), channel_id=1, source_target_pairs={{0,8},{1,9},{2,10},{3,11},{4,12},{5,13},{6,14},{7,15},{8,16},{9,17... | collective-permute-start | bytes 786440 | tf_op jit(solution)/shard_map/ppermute | solution.py:232
  7.1 1.0 %slice_bitcast_fusion = bf16[1024,128]{1,0:T(8,128)(2,1)S(1)} fusion(bf16[1,1,1280,128]{3,2,1,0:T(8,128)(2,1)} %param.5), kind=kLoop, calls=%fused_computation | loop fusion | bytes 524288 | tf_op jit(solution)/shard_map/slice | solution.py:233
  8.0 7.3 %collective-permute-start.1 = (bf16[1024,128]{1,0:T(8,128)(2,1)S(1)}, bf16[1024,128]{1,0:T(8,128)(2,1)S(1)}, u32[]{:S(2)}, u32[]{:S(2)}) collective-permute-start(bf16[1024,128]{1,0:T(8,128)(2,1)S(1)} %slice_bitcast_fusion), channel_id=1, source_target_pairs={{0,8},{1,9},{2,10},{3,11},{4,12},{5,13},{6,14},{7,15},{8,16},{9,17... | collective-permute-start | bytes 786440 | tf_op jit(solution)/shard_map/ppermute | solution.py:233
  15.4 7.0 %shard_map.37 = (bf16[1280,256]{1,0:T(8,128)(2,1)}, f32[2,1024,128]{2,1,0:T(8,128)}, f32[2,1024,128]{2,1,0:T(8,128)}) custom-call(bf16[1280,256]{1,0:T(8,128)(2,1)} %bitcast.11, bf16[1280,128]{1,0:T(8,128)(2,1)} %bitcast.9, bf16[1280,128]{1,0:T(8,128)(2,1)} %bitcast.10), custom_call_target="tpu_custom_call" | custom-call | flops 1677721600 | bytes 3407872 | tf_op jit(solution)/shard_map/pallas_call | solution.py:125
  22.4 11.2 %collective-permute-done.key_ref = bf16[1024,128]{1,0:T(8,128)(2,1)S(1)} collective-permute-done((bf16[1024,128]{1,0:T(8,128)(2,1)S(1)}, bf16[1024,128]{1,0:T(8,128)(2,1)S(1)}, u32[]{:S(2)}, u32[]{:S(2)}) %collective-permute-start) | collective-permute-done | bytes 262176 | tf_op jit(solution)/shard_map/ppermute | solution.py:232
  33.7 0.0 copy-start.1
  33.7 0.7 %copy-done.1 = bf16[1024,128]{1,0:T(8,128)(2,1)} copy-done((bf16[1024,128]{1,0:T(8,128)(2,1)}, bf16[1024,128]{1,0:T(8,128)(2,1)S(1)}, u32[]{:S(2)}) %copy-start.1) | copy-done | bytes 262168
  34.4 7.7 %shard_map.38 = (bf16[2,256,2560]{2,1,0:T(8,128)(2,1)}, f32[2,1024,128]{2,1,0:T(8,128)}) custom-call(s32[1]{0:T(128)} %bitcast.opening_ref, bf16[1280,256]{1,0:T(8,128)(2,1)} %bitcast.12, bf16[1024,128]{1,0:T(8,128)(2,1)} %copy-done.1, f32[2,1024,128]{2,1,0:T(8,128)} %get-tuple-element.10.stats_ref), custom_call_target="tpu_custom_call" | custom-call | flops 335544320 | bytes 5373952 | tf_op jit(solution)/shard_map/pallas_call | solution.py:157
  42.1 3.2 %collective-permute-done.1.value_ref = bf16[1024,128]{1,0:T(8,128)(2,1)S(1)} collective-permute-done((bf16[1024,128]{1,0:T(8,128)(2,1)S(1)}, bf16[1024,128]{1,0:T(8,128)(2,1)S(1)}, u32[]{:S(2)}, u32[]{:S(2)}) %collective-permute-start.1) | collective-permute-done | bytes 262176 | tf_op jit(solution)/shard_map/ppermute | solution.py:233
  45.3 0.0 copy-start
  45.3 0.7 %copy-done = bf16[1024,128]{1,0:T(8,128)(2,1)} copy-done((bf16[1024,128]{1,0:T(8,128)(2,1)}, bf16[1024,128]{1,0:T(8,128)(2,1)S(1)}, u32[]{:S(2)}) %copy-start) | copy-done | bytes 262168
  46.0 3.6 %shard_map.39 = bf16[1280,256]{1,0:T(8,128)(2,1)} custom-call(s32[1]{0:T(128)} %bitcast.opening_ref, bf16[2,256,2560]{2,1,0:T(8,128)(2,1)} %get-tuple-element.11.weight_ref, bf16[1024,128]{1,0:T(8,128)(2,1)} %copy-done, f32[2,1024,128]{2,1,0:T(8,128)} %get-tuple-element.12.merged_ref, ...), custom_call_target="tpu_custom_call", output_to_operand_aliasing={{}: (5, {})} | custom-call | flops 335544320 | bytes 6029312 | tf_op jit(solution)/shard_map/pallas_call | solution.py:189
Async XLA Ops:
  1.0 32.7 %collective-permute-start = (bf16[1024,128]{1,0:T(8,128)(2,1)S(1)}, bf16[1024,128]{1,0:T(8,128)(2,1)S(1)}, u32[]{:S(2)}, u32[]{:S(2)}) collective-permute-start(bf16[1024,128]{1,0:T(8,128)(2,1)S(1)} %slice_bitcast_fusion.1), channel_id=1, source_target_pairs={{0,8},{1,9},{2,10},{3,11},{4,12},{5,13},{6,14},{7,15},{8,16},{9,17... | collective-permute-start | bytes 786440 | tf_op jit(solution)/shard_map/ppermute | solution.py:232
  8.0 37.2 %collective-permute-start.1 = (bf16[1024,128]{1,0:T(8,128)(2,1)S(1)}, bf16[1024,128]{1,0:T(8,128)(2,1)S(1)}, u32[]{:S(2)}, u32[]{:S(2)}) collective-permute-start(bf16[1024,128]{1,0:T(8,128)(2,1)S(1)} %slice_bitcast_fusion), channel_id=1, source_target_pairs={{0,8},{1,9},{2,10},{3,11},{4,12},{5,13},{6,14},{7,15},{8,16},{9,17... | collective-permute-start | bytes 786440 | tf_op jit(solution)/shard_map/ppermute | solution.py:233
  33.7 0.7 %copy-start.1 = (bf16[1024,128]{1,0:T(8,128)(2,1)}, bf16[1024,128]{1,0:T(8,128)(2,1)S(1)}, u32[]{:S(2)}) copy-start(bf16[1024,128]{1,0:T(8,128)(2,1)S(1)} %collective-permute-done.key_ref) | copy-start | bytes 786436
  45.3 0.7 %copy-start = (bf16[1024,128]{1,0:T(8,128)(2,1)}, bf16[1024,128]{1,0:T(8,128)(2,1)S(1)}, u32[]{:S(2)}) copy-start(bf16[1024,128]{1,0:T(8,128)(2,1)S(1)} %collective-permute-done.1.value_ref) | copy-start | bytes 786436

commit v8 on v7

--- a/solution.py
+++ b/solution.py
@@ -94,18 +94,29 @@
         merged_ref[first_row:high_row, :] = packed_stats(rescale, row_total)
 
 
-def gather_kernel(opening_ref, weight_ref, value_ref, merged_ref, acc_ref, _, out_ref):
+def gather_kernel(opening_ref, weight_ref, low_ref, high_ref, merged_ref, acc_ref, _, out_ref):
     halo_rows = merged_ref.shape[0]
-    window = value_ref.shape[0]
+    split = low_ref.shape[0]
+    window = split + high_ref.shape[0]
     shut = opening_ref[0] != 0
     column = 0
     for first_row in range(0, halo_rows, QUERY_TILE):
         high_row = first_row + QUERY_TILE
         rescale, row_total, local_context = read_stats(merged_ref, acc_ref, first_row, QUERY_TILE)
-        width = window - first_row
-        context = jnp.dot(
+        context = 0.0
+        if first_row < split:
+            width = split - first_row
+            context = context + jnp.dot(
+                weight_ref[:, column : column + width],
+                low_ref[first_row:split, :],
+                preferred_element_type=jnp.float32,
+            )
+            column += width
+        start = max(first_row, split) - split
+        width = window - split - start
+        context = context + jnp.dot(
             weight_ref[:, column : column + width],
-            value_ref[first_row:window, :],
+            high_ref[start:, :],
             preferred_element_type=jnp.float32,
         )
         column += width
@@ -175,14 +186,15 @@
     )(opening, query_local, halo_keys, stats)
 
 
-def gather_part(opening, weights, halo_values, merged, acc, partial_out):
+def gather_part(opening, weights, low_values, high_values, merged, acc, partial_out):
     row_count, width = partial_out.shape
-    window, head_size = halo_values.shape
+    split, head_size = low_values.shape
     heads = width // head_size
     halo_rows = merged.shape[1]
     weight_width = weights.shape[2]
     column = pl.BlockSpec((halo_rows, head_size), lambda p, o: (0, p))
-    halo_block = pl.BlockSpec((window, head_size), lambda p, o: (0, 0))
+    low_block = pl.BlockSpec((split, head_size), lambda p, o: (0, 0))
+    high_block = pl.BlockSpec(high_values.shape, lambda p, o: (0, 0))
     stat_block = pl.BlockSpec((None, halo_rows, LANES), lambda p, o: (p, 0, 0))
     acc_block = pl.BlockSpec((None, halo_rows, head_size), lambda p, o: (p, 0, 0))
     weight_block = pl.BlockSpec((None, QUERY_TILE, weight_width), lambda p, o: (p, 0, 0))
@@ -193,7 +205,8 @@
             grid=(heads,),
             in_specs=[
                 weight_block,
-                halo_block,
+                low_block,
+                high_block,
                 stat_block,
                 acc_block,
                 pl.BlockSpec(memory_space=pl.ANY),
@@ -201,14 +214,14 @@
             out_specs=column,
         ),
         out_shape=jax.ShapeDtypeStruct((row_count, width), partial_out.dtype),
-        input_output_aliases={5: 0},
+        input_output_aliases={6: 0},
         cost_estimate=pl.CostEstimate(
             flops=2 * heads * QUERY_TILE * weight_width * head_size,
             transcendentals=0,
             bytes_accessed=2 * heads * QUERY_TILE * weight_width + 2 * row_count * width * 2
             + 8 * heads * halo_rows * LANES,
         ),
-    )(opening, weights, halo_values, merged, acc, partial_out)
+    )(opening, weights, low_values, high_values, merged, acc, partial_out)
 
 
 def per_device(queries, key_rows, value_rows):
@@ -230,11 +243,13 @@
             elif s > 0:
                 route.append(((s - 1) * model_count + (blocks - 1) * KVH + m, s * model_count + m))
     halo_keys = lax.ppermute(key_local[row_count - WINDOW :], ("seq", "mp"), route)
-    halo_values = lax.ppermute(value_local[row_count - WINDOW :], ("seq", "mp"), route)
+    split_row = row_count - WINDOW // 2
+    high_values = lax.ppermute(value_local[split_row:], ("seq", "mp"), route)
+    low_values = lax.ppermute(value_local[row_count - WINDOW : split_row], ("seq", "mp"), route)
     halo_rows = WINDOW
     partial_out, stats, acc = local_part(query_local, key_local, value_local, halo_rows)
     weights, merged = weigh_part(opening, query_local, halo_keys, stats)
-    attended = gather_part(opening, weights, halo_values, merged, acc, partial_out)
+    attended = gather_part(opening, weights, low_values, high_values, merged, acc, partial_out)
     return attended.reshape(1, 1, row_count, queries.shape[3])
 
 

time: 49.8 us -> 49.3 us (0.990); the launches traced: 49.6 us -> 48.4 us
  waiting for transfers between devices: 14.4 us -> 7.19 us
  starting transfers between devices: 13.4 us -> 19.5 us
    ppermute x1, waiting for transfers between devices: 11.2 us -> 4.83 us  [per_device(): lax.ppermute(key_local[row_count - WINDOW:], ('seq', 'mp'), route)]
    ppermute x1 -> x2, starting transfers between devices: 7.3 us -> 13.4 us  [the longest x1 7.3 us: per_device(): lax.ppermute(value_local[row_count - WINDOW:split_row], ('seq', 'mp'), ro...]
    ppermute x1 -> x2, waiting for transfers between devices: 3.18 us -> 2.36 us  [the longest x1 2.36 us: per_device(): high_values = lax.ppermute(value_local[split_row:], ('seq', 'mp'), route)]
    unnamed x4 -> x6, local copies, waits for them, and re-layouts: 1.41 us -> 1.34 us
  transfers between devices with their start and end apart: 2 -> 3, of which waited for: 2 -> 2; matrix products, arithmetic and copies ran while one was open for 2% -> 2% of each run, Pallas kernels for 30% -> 31%
where the time goes in v8:
time: 49.3 us; the launch traced here: 48.4 us
  starting transfers between devices  19.5 us (40%)
  Pallas kernels  18.4 us (37%)
  waiting for transfers between devices  7.19 us (15%)
  local copies, waits for them, and re-layouts  3.3 us (7%)
    pallas_call x1, Pallas kernels, weigh_part(): pl.pallas_call(weigh_kernel, grid_spec=pltpu.PrefetchScalarGridSpec(num_s...  7.75 us
    ppermute x1, starting transfers between devices, per_device(): lax.ppermute(value_local[row_count - WINDOW:split_row], ('seq', 'mp'), ro...  7.3 us
    pallas_call x1, Pallas kernels, local_part(): pl.pallas_call(local_kernel, grid=(heads,), in_specs=[head_block, whole,...  7.03 us
    ppermute x1, starting transfers between devices, per_device(): lax.ppermute(key_local[row_count - WINDOW:], ('seq', 'mp'), route)  6.09 us
    ppermute x1, starting transfers between devices, per_device(): high_values = lax.ppermute(value_local[split_row:], ('seq', 'mp'), route)  6.09 us
    ppermute x1, waiting for transfers between devices, per_device(): lax.ppermute(key_local[row_count - WINDOW:], ('seq', 'mp'), route)  4.83 us
    pallas_call x1, Pallas kernels, gather_part(): pl.pallas_call(gather_kernel, grid_spec=pltpu.PrefetchScalarGridSpec(num_...  3.59 us
    ppermute x1, waiting for transfers between devices, per_device(): high_values = lax.ppermute(value_local[split_row:], ('seq', 'mp'), route)  2.36 us
  transfers between devices with their start and end apart: 3, of which 2 were waited for; matrix products, arithmetic and copies ran while one was open for 2% of the time, Pallas kernels for 31%

profile of v8, /device:TPU:6, one launch (start us, length us, event | category | flops | bytes accessed | tf_op | source)
XLA Modules:
  0.0 48.4 jit_solution(5712120730617473183)
XLA Ops:
  0.0 1.0 %slice_bitcast_fusion = bf16[1024,128]{1,0:T(8,128)(2,1)S(1)} fusion(bf16[1,1,1280,128]{3,2,1,0:T(8,128)(2,1)} %param.4), kind=kLoop, calls=%fused_computation | loop fusion | bytes 524288 | tf_op jit(solution)/shard_map/slice | solution.py:245
  1.0 6.1 %collective-permute-start = (bf16[1024,128]{1,0:T(8,128)(2,1)S(1)}, bf16[1024,128]{1,0:T(8,128)(2,1)S(1)}, u32[]{:S(2)}, u32[]{:S(2)}) collective-permute-start(bf16[1024,128]{1,0:T(8,128)(2,1)S(1)} %slice_bitcast_fusion), channel_id=1, source_target_pairs={{0,8},{1,9},{2,10},{3,11},{4,12},{5,13},{6,14},{7,15},{8,16},{9,17... | collective-permute-start | bytes 786440 | tf_op jit(solution)/shard_map/ppermute | solution.py:245
  7.1 1.0 %slice_bitcast_fusion.1 = (bf16[512,128]{1,0:T(8,128)(2,1)S(1)}, bf16[512,128]{1,0:T(8,128)(2,1)S(1)}) fusion(bf16[1,1,1280,128]{3,2,1,0:T(8,128)(2,1)} %param.5), kind=kLoop, calls=%fused_computation.1 | loop fusion | bytes 524288 | tf_op jit(solution)/shard_map/slice | solution.py:247
  8.1 7.3 %collective-permute-start.1 = (bf16[512,128]{1,0:T(8,128)(2,1)S(1)}, bf16[512,128]{1,0:T(8,128)(2,1)S(1)}, u32[]{:S(2)}, u32[]{:S(2)}) collective-permute-start(bf16[512,128]{1,0:T(8,128)(2,1)S(1)} %get-tuple-element.16), channel_id=1, source_target_pairs={{0,8},{1,9},{2,10},{3,11},{4,12},{5,13},{6,14},{7,15},{8,16},{9,17... | collective-permute-start | bytes 393224 | tf_op jit(solution)/shard_map/ppermute | solution.py:248
  15.4 6.1 %collective-permute-start.2 = (bf16[512,128]{1,0:T(8,128)(2,1)S(1)}, bf16[512,128]{1,0:T(8,128)(2,1)S(1)}, u32[]{:S(2)}, u32[]{:S(2)}) collective-permute-start(bf16[512,128]{1,0:T(8,128)(2,1)S(1)} %get-tuple-element.15), channel_id=1, source_target_pairs={{0,8},{1,9},{2,10},{3,11},{4,12},{5,13},{6,14},{7,15},{8,16},{9,17... | collective-permute-start | bytes 393224 | tf_op jit(solution)/shard_map/ppermute | solution.py:247
  21.5 7.0 %shard_map.37 = (bf16[1280,256]{1,0:T(8,128)(2,1)}, f32[2,1024,128]{2,1,0:T(8,128)}, f32[2,1024,128]{2,1,0:T(8,128)}) custom-call(bf16[1280,256]{1,0:T(8,128)(2,1)} %bitcast.13, bf16[1280,128]{1,0:T(8,128)(2,1)} %bitcast.11, bf16[1280,128]{1,0:T(8,128)(2,1)} %bitcast.12), custom_call_target="tpu_custom_call" | custom-call | flops 1677721600 | bytes 3407872 | tf_op jit(solution)/shard_map/pallas_call | solution.py:136
  28.5 4.8 %collective-permute-done.key_ref = bf16[1024,128]{1,0:T(8,128)(2,1)S(1)} collective-permute-done((bf16[1024,128]{1,0:T(8,128)(2,1)S(1)}, bf16[1024,128]{1,0:T(8,128)(2,1)S(1)}, u32[]{:S(2)}, u32[]{:S(2)}) %collective-permute-start) | collective-permute-done | bytes 262176 | tf_op jit(solution)/shard_map/ppermute | solution.py:245
  33.4 0.0 copy-start.2
  33.4 0.7 %copy-done.2 = bf16[1024,128]{1,0:T(8,128)(2,1)} copy-done((bf16[1024,128]{1,0:T(8,128)(2,1)}, bf16[1024,128]{1,0:T(8,128)(2,1)S(1)}, u32[]{:S(2)}) %copy-start.2) | copy-done | bytes 262168
  34.1 7.7 %shard_map.38 = (bf16[2,256,2560]{2,1,0:T(8,128)(2,1)}, f32[2,1024,128]{2,1,0:T(8,128)}) custom-call(s32[1]{0:T(128)} %bitcast.opening_ref, bf16[1280,256]{1,0:T(8,128)(2,1)} %bitcast.14, bf16[1024,128]{1,0:T(8,128)(2,1)} %copy-done.2, f32[2,1024,128]{2,1,0:T(8,128)} %get-tuple-element.10.stats_ref), custom_call_target="tpu_custom_call" | custom-call | flops 335544320 | bytes 5373952 | tf_op jit(solution)/shard_map/pallas_call | solution.py:168
  41.8 0.0 collective-permute-done.1.low_ref
  41.8 0.0 copy-start
  41.8 2.4 %collective-permute-done.2.high_ref = bf16[512,128]{1,0:T(8,128)(2,1)S(1)} collective-permute-done((bf16[512,128]{1,0:T(8,128)(2,1)S(1)}, bf16[512,128]{1,0:T(8,128)(2,1)S(1)}, u32[]{:S(2)}, u32[]{:S(2)}) %collective-permute-start.2) | collective-permute-done | bytes 131104 | tf_op jit(solution)/shard_map/ppermute | solution.py:247
  44.2 0.0 copy-start.1
  44.2 0.0 copy-done
  44.2 0.6 %copy-done.1 = bf16[512,128]{1,0:T(8,128)(2,1)} copy-done((bf16[512,128]{1,0:T(8,128)(2,1)}, bf16[512,128]{1,0:T(8,128)(2,1)S(1)}, u32[]{:S(2)}) %copy-start.1) | copy-done | bytes 131096
  44.8 3.6 %shard_map.39 = bf16[1280,256]{1,0:T(8,128)(2,1)} custom-call(s32[1]{0:T(128)} %bitcast.opening_ref, bf16[2,256,2560]{2,1,0:T(8,128)(2,1)} %get-tuple-element.11.weight_ref, bf16[512,128]{1,0:T(8,128)(2,1)} %copy-done, bf16[512,128]{1,0:T(8,128)(2,1)} %copy-done.1, f32[2,1024,128]{2,1,0:T(8,128)} %get-tuple-element.12.merged_ref, ...), custom_call_target="tpu_custom_call", output_to_operand_aliasing={{}: (6, {})} | custom-call | flops 335544320 | bytes 6029312 | tf_op jit(solution)/shard_map/pallas_call | solution.py:201
Async XLA Ops:
  1.0 32.4 %collective-permute-start = (bf16[1024,128]{1,0:T(8,128)(2,1)S(1)}, bf16[1024,128]{1,0:T(8,128)(2,1)S(1)}, u32[]{:S(2)}, u32[]{:S(2)}) collective-permute-start(bf16[1024,128]{1,0:T(8,128)(2,1)S(1)} %slice_bitcast_fusion), channel_id=1, source_target_pairs={{0,8},{1,9},{2,10},{3,11},{4,12},{5,13},{6,14},{7,15},{8,16},{9,17... | collective-permute-start | bytes 786440 | tf_op jit(solution)/shard_map/ppermute | solution.py:245
  8.1 33.7 %collective-permute-start.1 = (bf16[512,128]{1,0:T(8,128)(2,1)S(1)}, bf16[512,128]{1,0:T(8,128)(2,1)S(1)}, u32[]{:S(2)}, u32[]{:S(2)}) collective-permute-start(bf16[512,128]{1,0:T(8,128)(2,1)S(1)} %get-tuple-element.16), channel_id=1, source_target_pairs={{0,8},{1,9},{2,10},{3,11},{4,12},{5,13},{6,14},{7,15},{8,16},{9,17... | collective-permute-start | bytes 393224 | tf_op jit(solution)/shard_map/ppermute | solution.py:248
  15.4 28.8 %collective-permute-start.2 = (bf16[512,128]{1,0:T(8,128)(2,1)S(1)}, bf16[512,128]{1,0:T(8,128)(2,1)S(1)}, u32[]{:S(2)}, u32[]{:S(2)}) collective-permute-start(bf16[512,128]{1,0:T(8,128)(2,1)S(1)} %get-tuple-element.15), channel_id=1, source_target_pairs={{0,8},{1,9},{2,10},{3,11},{4,12},{5,13},{6,14},{7,15},{8,16},{9,17... | collective-permute-start | bytes 393224 | tf_op jit(solution)/shard_map/ppermute | solution.py:247
  33.4 0.7 %copy-start.2 = (bf16[1024,128]{1,0:T(8,128)(2,1)}, bf16[1024,128]{1,0:T(8,128)(2,1)S(1)}, u32[]{:S(2)}) copy-start(bf16[1024,128]{1,0:T(8,128)(2,1)S(1)} %collective-permute-done.key_ref) | copy-start | bytes 786436
  41.8 2.4 %copy-start = (bf16[512,128]{1,0:T(8,128)(2,1)}, bf16[512,128]{1,0:T(8,128)(2,1)S(1)}, u32[]{:S(2)}) copy-start(bf16[512,128]{1,0:T(8,128)(2,1)S(1)} %collective-permute-done.1.low_ref) | copy-start | bytes 393220
  44.2 0.6 %copy-start.1 = (bf16[512,128]{1,0:T(8,128)(2,1)}, bf16[512,128]{1,0:T(8,128)(2,1)S(1)}, u32[]{:S(2)}) copy-start(bf16[512,128]{1,0:T(8,128)(2,1)S(1)} %collective-permute-done.2.high_ref) | copy-start | bytes 393220

commit v9 on v5

--- a/solution.py
+++ b/solution.py
@@ -94,22 +94,31 @@
         merged_ref[first_row:high_row, :] = packed_stats(rescale, row_total)
 
 
-def gather_kernel(opening_ref, weight_ref, value_ref, merged_ref, acc_ref, partial_ref, out_ref):
+def gather_kernel(opening_ref, weight_ref, *refs):
+    piece_refs = refs[:-4]
+    merged_ref, acc_ref, _, out_ref = refs[-4:]
     halo_rows = merged_ref.shape[0]
-    window = value_ref.shape[0]
     shut = opening_ref[0] != 0
-    out_ref[halo_rows:, :] = partial_ref[halo_rows:, :]
+    bounds = [0]
+    for piece_ref in piece_refs:
+        bounds.append(bounds[-1] + piece_ref.shape[0])
     column = 0
     for first_row in range(0, halo_rows, QUERY_TILE):
         high_row = first_row + QUERY_TILE
         rescale, row_total, local_context = read_stats(merged_ref, acc_ref, first_row, QUERY_TILE)
-        width = window - first_row
-        context = jnp.dot(
-            weight_ref[:, column : column + width],
-            value_ref[first_row:window, :],
-            preferred_element_type=jnp.float32,
-        )
-        column += width
+        context = 0.0
+        for index, piece_ref in enumerate(piece_refs):
+            low, high = bounds[index], bounds[index + 1]
+            start = max(low, first_row)
+            if start >= high:
+                continue
+            width = high - start
+            context = context + jnp.dot(
+                weight_ref[:, column : column + width],
+                piece_ref[start - low :, :],
+                preferred_element_type=jnp.float32,
+            )
+            column += width
         context = rescale * local_context + jnp.where(shut, 0.0, context)
         out_ref[first_row:high_row, :] = (context / row_total).astype(out_ref.dtype)
 
@@ -176,14 +185,14 @@
     )(opening, query_local, halo_keys, stats)
 
 
-def gather_part(opening, weights, halo_values, merged, acc, partial_out):
+def gather_part(opening, weights, pieces, merged, acc, partial_out):
     row_count, width = partial_out.shape
-    window, head_size = halo_values.shape
+    head_size = pieces[0].shape[1]
     heads = width // head_size
     halo_rows = merged.shape[1]
     weight_width = weights.shape[2]
-    column = pl.BlockSpec((row_count, head_size), lambda p, o: (0, p))
-    halo_block = pl.BlockSpec((window, head_size), lambda p, o: (0, 0))
+    column = pl.BlockSpec((halo_rows, head_size), lambda p, o: (0, p))
+    piece_blocks = [pl.BlockSpec(piece.shape, lambda p, o: (0, 0)) for piece in pieces]
     stat_block = pl.BlockSpec((None, halo_rows, LANES), lambda p, o: (p, 0, 0))
     acc_block = pl.BlockSpec((None, halo_rows, head_size), lambda p, o: (p, 0, 0))
     weight_block = pl.BlockSpec((None, QUERY_TILE, weight_width), lambda p, o: (p, 0, 0))
@@ -192,18 +201,19 @@
         grid_spec=pltpu.PrefetchScalarGridSpec(
             num_scalar_prefetch=1,
             grid=(heads,),
-            in_specs=[weight_block, halo_block, stat_block, acc_block, column],
+            in_specs=[weight_block, *piece_blocks, stat_block, acc_block,
+                      pl.BlockSpec(memory_space=pl.ANY)],
             out_specs=column,
         ),
         out_shape=jax.ShapeDtypeStruct((row_count, width), partial_out.dtype),
-        input_output_aliases={5: 0},
+        input_output_aliases={4 + len(pieces): 0},
         cost_estimate=pl.CostEstimate(
             flops=2 * heads * QUERY_TILE * weight_width * head_size,
             transcendentals=0,
             bytes_accessed=2 * heads * QUERY_TILE * weight_width + 2 * row_count * width * 2
             + 8 * heads * halo_rows * LANES,
         ),
-    )(opening, weights, halo_values, merged, acc, partial_out)
+    )(opening, weights, *pieces, merged, acc, partial_out)
 
 
 def per_device(queries, key_rows, value_rows):
@@ -225,11 +235,16 @@
             elif s > 0:
                 route.append(((s - 1) * model_count + (blocks - 1) * KVH + m, s * model_count + m))
     halo_keys = lax.ppermute(key_local[row_count - WINDOW :], ("seq", "mp"), route)
-    halo_values = lax.ppermute(value_local[row_count - WINDOW :], ("seq", "mp"), route)
+    first = row_count - WINDOW
+    cuts = [first, first + 384, first + 640, row_count]
+    pieces = [
+        lax.ppermute(value_local[cuts[i] : cuts[i + 1]], ("seq", "mp"), route)
+        for i in (2, 1, 0)
+    ][::-1]
     halo_rows = WINDOW
     partial_out, stats, acc = local_part(query_local, key_local, value_local, halo_rows)
     weights, merged = weigh_part(opening, query_local, halo_keys, stats)
-    attended = gather_part(opening, weights, halo_values, merged, acc, partial_out)
+    attended = gather_part(opening, weights, pieces, merged, acc, partial_out)
     return attended.reshape(1, 1, row_count, queries.shape[3])
 
 

time: 50 us -> 49.5 us (0.990); the launches traced: 49.8 us -> 48.7 us
  waiting for transfers between devices: 14.4 us -> 1.68 us
  starting transfers between devices: 13.4 us -> 24.4 us
  local copies, waits for them, and re-layouts: 3.35 us -> 4.18 us
    ppermute x1, waiting for transfers between devices: 11.2 us -> 0.01 us  [per_device(): lax.ppermute(key_local[row_count - WINDOW:], ('seq', 'mp'), route)]
    ppermute x1 -> x3, starting transfers between devices: 7.3 us -> 18.3 us  [per_device(): lax.ppermute(value_local[cuts[i]:cuts[i + 1]], ('seq', 'mp'), route)]
    ppermute x1 -> x3, waiting for transfers between devices: 3.18 us -> 1.67 us  [per_device(): lax.ppermute(value_local[cuts[i]:cuts[i + 1]], ('seq', 'mp'), route)]
    slice x1 -> x2, local copies, waits for them, and re-layouts: 0.97 us -> 1.81 us  [per_device(): value_local[cuts[i]:cuts[i + 1]]]
    unnamed x4 -> x8, local copies, waits for them, and re-layouts: 1.41 us -> 1.41 us
  transfers between devices with their start and end apart: 2 -> 4, of which waited for: 2 -> 1; matrix products, arithmetic and copies ran while one was open for 2% -> 4% of each run, Pallas kernels for 30% -> 30%
where the time goes in v9:
time: 49.5 us; the launch traced here: 48.7 us
  starting transfers between devices  24.4 us (49%)
  Pallas kernels  18.4 us (37%)
  local copies, waits for them, and re-layouts  4.18 us (8%)
  waiting for transfers between devices  1.68 us (3%)
    ppermute x3, starting transfers between devices, per_device(): lax.ppermute(value_local[cuts[i]:cuts[i + 1]], ('seq', 'mp'), route)  18.3 us
    pallas_call x1, Pallas kernels, weigh_part(): pl.pallas_call(weigh_kernel, grid_spec=pltpu.PrefetchScalarGridSpec(num_s...  7.76 us
    pallas_call x1, Pallas kernels, local_part(): pl.pallas_call(local_kernel, grid=(heads,), in_specs=[head_block, whole,...  7.03 us
    ppermute x1, starting transfers between devices, per_device(): lax.ppermute(key_local[row_count - WINDOW:], ('seq', 'mp'), route)  6.09 us
    pallas_call x1, Pallas kernels, gather_part(): pl.pallas_call(gather_kernel, grid_spec=pltpu.PrefetchScalarGridSpec(num_...  3.59 us
    slice x2, local copies, waits for them, and re-layouts, per_device(): value_local[cuts[i]:cuts[i + 1]]  1.81 us
    ppermute x3, waiting for transfers between devices, per_device(): lax.ppermute(value_local[cuts[i]:cuts[i + 1]], ('seq', 'mp'), route)  1.67 us
    unnamed x8, local copies, waits for them, and re-layouts  1.41 us
  transfers between devices with their start and end apart: 4, of which 1 were waited for; matrix products, arithmetic and copies ran while one was open for 4% of the time, Pallas kernels for 30%

profile of v9, /device:TPU:6, one launch (start us, length us, event | category | flops | bytes accessed | tf_op | source)
XLA Modules:
  0.0 48.7 jit_solution(16223680183680457514)
XLA Ops:
  0.0 1.0 %slice_bitcast_fusion = bf16[1024,128]{1,0:T(8,128)(2,1)S(1)} fusion(bf16[1,1,1280,128]{3,2,1,0:T(8,128)(2,1)} %param.4), kind=kLoop, calls=%fused_computation | loop fusion | bytes 524288 | tf_op jit(solution)/shard_map/slice | solution.py:237
  1.0 6.1 %collective-permute-start = (bf16[1024,128]{1,0:T(8,128)(2,1)S(1)}, bf16[1024,128]{1,0:T(8,128)(2,1)S(1)}, u32[]{:S(2)}, u32[]{:S(2)}) collective-permute-start(bf16[1024,128]{1,0:T(8,128)(2,1)S(1)} %slice_bitcast_fusion), channel_id=1, source_target_pairs={{0,8},{1,9},{2,10},{3,11},{4,12},{5,13},{6,14},{7,15},{8,16},{9,17... | collective-permute-start | bytes 786440 | tf_op jit(solution)/shard_map/ppermute | solution.py:237
  7.1 1.0 %slice_bitcast_fusion.1 = (bf16[384,128]{1,0:T(8,128)(2,1)S(1)}, bf16[384,128]{1,0:T(8,128)(2,1)S(1)}) fusion(bf16[1,1,1280,128]{3,2,1,0:T(8,128)(2,1)} %param.5), kind=kLoop, calls=%fused_computation.1 | loop fusion | bytes 393216 | tf_op jit(solution)/shard_map/slice | solution.py:241
  8.0 7.3 %collective-permute-start.1 = (bf16[384,128]{1,0:T(8,128)(2,1)S(1)}, bf16[384,128]{1,0:T(8,128)(2,1)S(1)}, u32[]{:S(2)}, u32[]{:S(2)}) collective-permute-start(bf16[384,128]{1,0:T(8,128)(2,1)S(1)} %get-tuple-element.16), channel_id=1, source_target_pairs={{0,8},{1,9},{2,10},{3,11},{4,12},{5,13},{6,14},{7,15},{8,16},{9,17... | collective-permute-start | bytes 294920 | tf_op jit(solution)/shard_map/ppermute | solution.py:241
  15.3 6.1 %collective-permute-start.3 = (bf16[384,128]{1,0:T(8,128)(2,1)S(1)}, bf16[384,128]{1,0:T(8,128)(2,1)S(1)}, u32[]{:S(2)}, u32[]{:S(2)}) collective-permute-start(bf16[384,128]{1,0:T(8,128)(2,1)S(1)} %get-tuple-element.15), channel_id=1, source_target_pairs={{0,8},{1,9},{2,10},{3,11},{4,12},{5,13},{6,14},{7,15},{8,16},{9,17... | collective-permute-start | bytes 294920 | tf_op jit(solution)/shard_map/ppermute | solution.py:241
  21.4 0.8 %slice_bitcast_fusion.3 = bf16[256,128]{1,0:T(8,128)(2,1)S(1)} fusion(bf16[1,1,1280,128]{3,2,1,0:T(8,128)(2,1)} %param.5), kind=kLoop, calls=%fused_computation.3 | loop fusion | bytes 131072 | tf_op jit(solution)/shard_map/slice | solution.py:241
  22.3 4.9 %collective-permute-start.2 = (bf16[256,128]{1,0:T(8,128)(2,1)S(1)}, bf16[256,128]{1,0:T(8,128)(2,1)S(1)}, u32[]{:S(2)}, u32[]{:S(2)}) collective-permute-start(bf16[256,128]{1,0:T(8,128)(2,1)S(1)} %slice_bitcast_fusion.3), channel_id=1, source_target_pairs={{0,8},{1,9},{2,10},{3,11},{4,12},{5,13},{6,14},{7,15},{8,16},{9,17... | collective-permute-start | bytes 196616 | tf_op jit(solution)/shard_map/ppermute | solution.py:241
  27.2 7.0 %shard_map.37 = (bf16[1280,256]{1,0:T(8,128)(2,1)}, f32[2,1024,128]{2,1,0:T(8,128)}, f32[2,1024,128]{2,1,0:T(8,128)}) custom-call(bf16[1280,256]{1,0:T(8,128)(2,1)} %bitcast.15, bf16[1280,128]{1,0:T(8,128)(2,1)} %bitcast.14, bf16[1280,128]{1,0:T(8,128)(2,1)} %bitcast.13), custom_call_target="tpu_custom_call" | custom-call | flops 1677721600 | bytes 3407872 | tf_op jit(solution)/shard_map/pallas_call | solution.py:135
  34.2 0.0 collective-permute-done.key_ref
  34.2 0.0 copy-start.3
  34.2 0.7 %copy-done.3 = bf16[1024,128]{1,0:T(8,128)(2,1)} copy-done((bf16[1024,128]{1,0:T(8,128)(2,1)}, bf16[1024,128]{1,0:T(8,128)(2,1)S(1)}, u32[]{:S(2)}) %copy-start.3) | copy-done | bytes 262168
  34.9 7.8 %shard_map.38 = (bf16[2,256,2560]{2,1,0:T(8,128)(2,1)}, f32[2,1024,128]{2,1,0:T(8,128)}) custom-call(s32[1]{0:T(128)} %bitcast.opening_ref, bf16[1280,256]{1,0:T(8,128)(2,1)} %bitcast.16, bf16[1024,128]{1,0:T(8,128)(2,1)} %copy-done.3, f32[2,1024,128]{2,1,0:T(8,128)} %get-tuple-element.10.stats_ref), custom_call_target="tpu_custom_call" | custom-call | flops 335544320 | bytes 5373952 | tf_op jit(solution)/shard_map/pallas_call | solution.py:167
  42.7 1.7 %collective-permute-done.2.refs_1_ = bf16[256,128]{1,0:T(8,128)(2,1)S(1)} collective-permute-done((bf16[256,128]{1,0:T(8,128)(2,1)S(1)}, bf16[256,128]{1,0:T(8,128)(2,1)S(1)}, u32[]{:S(2)}, u32[]{:S(2)}) %collective-permute-start.2) | collective-permute-done | bytes 65568 | tf_op jit(solution)/shard_map/ppermute | solution.py:241
  44.4 0.0 copy-start.2
  44.4 0.0 collective-permute-done.1.refs_0_
  44.4 0.0 copy-start
  44.4 0.0 collective-permute-done.3.refs_2_
  44.4 0.0 copy-start.1
  44.4 0.6 %copy-done.2 = bf16[256,128]{1,0:T(8,128)(2,1)} copy-done((bf16[256,128]{1,0:T(8,128)(2,1)}, bf16[256,128]{1,0:T(8,128)(2,1)S(1)}, u32[]{:S(2)}) %copy-start.2) | copy-done | bytes 65560
  45.0 0.0 copy-done
  45.0 0.1 copy-done.1
  45.1 3.6 %shard_map.39 = bf16[1280,256]{1,0:T(8,128)(2,1)} custom-call(s32[1]{0:T(128)} %bitcast.opening_ref, bf16[2,256,2560]{2,1,0:T(8,128)(2,1)} %get-tuple-element.11.weight_ref, bf16[384,128]{1,0:T(8,128)(2,1)} %copy-done, bf16[256,128]{1,0:T(8,128)(2,1)} %copy-done.2, bf16[384,128]{1,0:T(8,128)(2,1)} %copy-done.1, ...), custom_call_target="tpu_custom_call", output_to_operand_aliasing={{}: (7, {})} | custom-call | flops 335544320 | bytes 6029312 | tf_op jit(solution)/shard_map/pallas_call | solution.py:199
Async XLA Ops:
  1.0 33.2 %collective-permute-start = (bf16[1024,128]{1,0:T(8,128)(2,1)S(1)}, bf16[1024,128]{1,0:T(8,128)(2,1)S(1)}, u32[]{:S(2)}, u32[]{:S(2)}) collective-permute-start(bf16[1024,128]{1,0:T(8,128)(2,1)S(1)} %slice_bitcast_fusion), channel_id=1, source_target_pairs={{0,8},{1,9},{2,10},{3,11},{4,12},{5,13},{6,14},{7,15},{8,16},{9,17... | collective-permute-start | bytes 786440 | tf_op jit(solution)/shard_map/ppermute | solution.py:237
  8.0 36.3 %collective-permute-start.1 = (bf16[384,128]{1,0:T(8,128)(2,1)S(1)}, bf16[384,128]{1,0:T(8,128)(2,1)S(1)}, u32[]{:S(2)}, u32[]{:S(2)}) collective-permute-start(bf16[384,128]{1,0:T(8,128)(2,1)S(1)} %get-tuple-element.16), channel_id=1, source_target_pairs={{0,8},{1,9},{2,10},{3,11},{4,12},{5,13},{6,14},{7,15},{8,16},{9,17... | collective-permute-start | bytes 294920 | tf_op jit(solution)/shard_map/ppermute | solution.py:241
  15.3 29.0 %collective-permute-start.3 = (bf16[384,128]{1,0:T(8,128)(2,1)S(1)}, bf16[384,128]{1,0:T(8,128)(2,1)S(1)}, u32[]{:S(2)}, u32[]{:S(2)}) collective-permute-start(bf16[384,128]{1,0:T(8,128)(2,1)S(1)} %get-tuple-element.15), channel_id=1, source_target_pairs={{0,8},{1,9},{2,10},{3,11},{4,12},{5,13},{6,14},{7,15},{8,16},{9,17... | collective-permute-start | bytes 294920 | tf_op jit(solution)/shard_map/ppermute | solution.py:241
  22.3 22.1 %collective-permute-start.2 = (bf16[256,128]{1,0:T(8,128)(2,1)S(1)}, bf16[256,128]{1,0:T(8,128)(2,1)S(1)}, u32[]{:S(2)}, u32[]{:S(2)}) collective-permute-start(bf16[256,128]{1,0:T(8,128)(2,1)S(1)} %slice_bitcast_fusion.3), channel_id=1, source_target_pairs={{0,8},{1,9},{2,10},{3,11},{4,12},{5,13},{6,14},{7,15},{8,16},{9,17... | collective-permute-start | bytes 196616 | tf_op jit(solution)/shard_map/ppermute | solution.py:241
  34.2 0.7 %copy-start.3 = (bf16[1024,128]{1,0:T(8,128)(2,1)}, bf16[1024,128]{1,0:T(8,128)(2,1)S(1)}, u32[]{:S(2)}) copy-start(bf16[1024,128]{1,0:T(8,128)(2,1)S(1)} %collective-permute-done.key_ref) | copy-start | bytes 786436
  44.4 0.6 %copy-start.2 = (bf16[256,128]{1,0:T(8,128)(2,1)}, bf16[256,128]{1,0:T(8,128)(2,1)S(1)}, u32[]{:S(2)}) copy-start(bf16[256,128]{1,0:T(8,128)(2,1)S(1)} %collective-permute-done.2.refs_1_) | copy-start | bytes 196612
  44.4 0.7 %copy-start = (bf16[384,128]{1,0:T(8,128)(2,1)}, bf16[384,128]{1,0:T(8,128)(2,1)S(1)}, u32[]{:S(2)}) copy-start(bf16[384,128]{1,0:T(8,128)(2,1)S(1)} %collective-permute-done.1.refs_0_) | copy-start | bytes 294916
  44.4 0.7 %copy-start.1 = (bf16[384,128]{1,0:T(8,128)(2,1)}, bf16[384,128]{1,0:T(8,128)(2,1)S(1)}, u32[]{:S(2)}) copy-start(bf16[384,128]{1,0:T(8,128)(2,1)S(1)} %collective-permute-done.3.refs_2_) | copy-start | bytes 294916

commit v10 on v8

--- a/solution.py
+++ b/solution.py
@@ -87,18 +87,19 @@
             probable = jnp.exp(scores - row_top)
             row_total = row_total + jnp.sum(probable, axis=1, keepdims=True)
             width = scores.shape[1]
-            weight_ref[:, column : column + width] = probable.astype(weight_ref.dtype)
+            weight_ref[:, column : column + width] = jnp.where(shut, 0.0, probable).astype(
+                weight_ref.dtype
+            )
             column += width
         rescale = jnp.where(shut, 1.0, rescale)
         row_total = jnp.where(shut, local_total, row_total)
         merged_ref[first_row:high_row, :] = packed_stats(rescale, row_total)
 
 
-def gather_kernel(opening_ref, weight_ref, low_ref, high_ref, merged_ref, acc_ref, _, out_ref):
+def gather_kernel(weight_ref, low_ref, high_ref, merged_ref, acc_ref, _, out_ref):
     halo_rows = merged_ref.shape[0]
     split = low_ref.shape[0]
     window = split + high_ref.shape[0]
-    shut = opening_ref[0] != 0
     column = 0
     for first_row in range(0, halo_rows, QUERY_TILE):
         high_row = first_row + QUERY_TILE
@@ -120,7 +121,7 @@
             preferred_element_type=jnp.float32,
         )
         column += width
-        context = rescale * local_context + jnp.where(shut, 0.0, context)
+        context = rescale * local_context + context
         out_ref[first_row:high_row, :] = (context / row_total).astype(out_ref.dtype)
 
 
@@ -186,22 +187,21 @@
     )(opening, query_local, halo_keys, stats)
 
 
-def gather_part(opening, weights, low_values, high_values, merged, acc, partial_out):
+def gather_part(weights, low_values, high_values, merged, acc, partial_out):
     row_count, width = partial_out.shape
     split, head_size = low_values.shape
     heads = width // head_size
     halo_rows = merged.shape[1]
     weight_width = weights.shape[2]
-    column = pl.BlockSpec((halo_rows, head_size), lambda p, o: (0, p))
-    low_block = pl.BlockSpec((split, head_size), lambda p, o: (0, 0))
-    high_block = pl.BlockSpec(high_values.shape, lambda p, o: (0, 0))
-    stat_block = pl.BlockSpec((None, halo_rows, LANES), lambda p, o: (p, 0, 0))
-    acc_block = pl.BlockSpec((None, halo_rows, head_size), lambda p, o: (p, 0, 0))
-    weight_block = pl.BlockSpec((None, QUERY_TILE, weight_width), lambda p, o: (p, 0, 0))
+    column = pl.BlockSpec((halo_rows, head_size), lambda p: (0, p))
+    low_block = pl.BlockSpec((split, head_size), lambda p: (0, 0))
+    high_block = pl.BlockSpec(high_values.shape, lambda p: (0, 0))
+    stat_block = pl.BlockSpec((None, halo_rows, LANES), lambda p: (p, 0, 0))
+    acc_block = pl.BlockSpec((None, halo_rows, head_size), lambda p: (p, 0, 0))
+    weight_block = pl.BlockSpec((None, QUERY_TILE, weight_width), lambda p: (p, 0, 0))
     return pl.pallas_call(
         gather_kernel,
-        grid_spec=pltpu.PrefetchScalarGridSpec(
-            num_scalar_prefetch=1,
+        grid_spec=pl.GridSpec(
             grid=(heads,),
             in_specs=[
                 weight_block,
@@ -214,14 +214,14 @@
             out_specs=column,
         ),
         out_shape=jax.ShapeDtypeStruct((row_count, width), partial_out.dtype),
-        input_output_aliases={6: 0},
+        input_output_aliases={5: 0},
         cost_estimate=pl.CostEstimate(
             flops=2 * heads * QUERY_TILE * weight_width * head_size,
             transcendentals=0,
             bytes_accessed=2 * heads * QUERY_TILE * weight_width + 2 * row_count * width * 2
             + 8 * heads * halo_rows * LANES,
         ),
-    )(opening, weights, low_values, high_values, merged, acc, partial_out)
+    )(weights, low_values, high_values, merged, acc, partial_out)
 
 
 def per_device(queries, key_rows, value_rows):
@@ -249,7 +249,7 @@
     halo_rows = WINDOW
     partial_out, stats, acc = local_part(query_local, key_local, value_local, halo_rows)
     weights, merged = weigh_part(opening, query_local, halo_keys, stats)
-    attended = gather_part(opening, weights, low_values, high_values, merged, acc, partial_out)
+    attended = gather_part(weights, low_values, high_values, merged, acc, partial_out)
     return attended.reshape(1, 1, row_count, queries.shape[3])
 
 

time: 49.3 us -> 49.3 us (level)
  no operation moved by 1% of the time
where the time goes in v10:
time: 49.3 us; the launch traced here: 48.4 us
  starting transfers between devices  19.5 us (40%)
  Pallas kernels  18.4 us (37%)
  waiting for transfers between devices  7.13 us (14%)
  local copies, waits for them, and re-layouts  3.3 us (7%)
    pallas_call x1, Pallas kernels, weigh_part(): pl.pallas_call(weigh_kernel, grid_spec=pltpu.PrefetchScalarGridSpec(num_s...  7.81 us
    ppermute x1, starting transfers between devices, per_device(): lax.ppermute(value_local[row_count - WINDOW:split_row], ('seq', 'mp'), ro...  7.3 us
    pallas_call x1, Pallas kernels, local_part(): pl.pallas_call(local_kernel, grid=(heads,), in_specs=[head_block, whole,...  7.03 us
    ppermute x1, starting transfers between devices, per_device(): lax.ppermute(key_local[row_count - WINDOW:], ('seq', 'mp'), route)  6.09 us
    ppermute x1, starting transfers between devices, per_device(): high_values = lax.ppermute(value_local[split_row:], ('seq', 'mp'), route)  6.09 us
    ppermute x1, waiting for transfers between devices, per_device(): lax.ppermute(key_local[row_count - WINDOW:], ('seq', 'mp'), route)  4.83 us
    pallas_call x1, Pallas kernels, gather_part(): pl.pallas_call(gather_kernel, grid_spec=pl.GridSpec(grid=(heads,), in_spe...  3.59 us
    ppermute x1, waiting for transfers between devices, per_device(): high_values = lax.ppermute(value_local[split_row:], ('seq', 'mp'), route)  2.29 us
  transfers between devices with their start and end apart: 3, of which 2 were waited for; matrix products, arithmetic and copies ran while one was open for 2% of the time, Pallas kernels for 31%

profile of v10, /device:TPU:6, one launch (start us, length us, event | category | flops | bytes accessed | tf_op | source)
XLA Modules:
  0.0 48.4 jit_solution(14247023314165124348)
XLA Ops:
  0.0 1.0 %slice_bitcast_fusion = bf16[1024,128]{1,0:T(8,128)(2,1)S(1)} fusion(bf16[1,1,1280,128]{3,2,1,0:T(8,128)(2,1)} %param.4), kind=kLoop, calls=%fused_computation | loop fusion | bytes 524288 | tf_op jit(solution)/shard_map/slice | solution.py:245
  1.0 6.1 %collective-permute-start = (bf16[1024,128]{1,0:T(8,128)(2,1)S(1)}, bf16[1024,128]{1,0:T(8,128)(2,1)S(1)}, u32[]{:S(2)}, u32[]{:S(2)}) collective-permute-start(bf16[1024,128]{1,0:T(8,128)(2,1)S(1)} %slice_bitcast_fusion), channel_id=1, source_target_pairs={{0,8},{1,9},{2,10},{3,11},{4,12},{5,13},{6,14},{7,15},{8,16},{9,17... | collective-permute-start | bytes 786440 | tf_op jit(solution)/shard_map/ppermute | solution.py:245
  7.1 1.0 %slice_bitcast_fusion.1 = (bf16[512,128]{1,0:T(8,128)(2,1)S(1)}, bf16[512,128]{1,0:T(8,128)(2,1)S(1)}) fusion(bf16[1,1,1280,128]{3,2,1,0:T(8,128)(2,1)} %param.5), kind=kLoop, calls=%fused_computation.1 | loop fusion | bytes 524288 | tf_op jit(solution)/shard_map/slice | solution.py:247
  8.1 7.3 %collective-permute-start.1 = (bf16[512,128]{1,0:T(8,128)(2,1)S(1)}, bf16[512,128]{1,0:T(8,128)(2,1)S(1)}, u32[]{:S(2)}, u32[]{:S(2)}) collective-permute-start(bf16[512,128]{1,0:T(8,128)(2,1)S(1)} %get-tuple-element.16), channel_id=1, source_target_pairs={{0,8},{1,9},{2,10},{3,11},{4,12},{5,13},{6,14},{7,15},{8,16},{9,17... | collective-permute-start | bytes 393224 | tf_op jit(solution)/shard_map/ppermute | solution.py:248
  15.4 6.1 %collective-permute-start.2 = (bf16[512,128]{1,0:T(8,128)(2,1)S(1)}, bf16[512,128]{1,0:T(8,128)(2,1)S(1)}, u32[]{:S(2)}, u32[]{:S(2)}) collective-permute-start(bf16[512,128]{1,0:T(8,128)(2,1)S(1)} %get-tuple-element.15), channel_id=1, source_target_pairs={{0,8},{1,9},{2,10},{3,11},{4,12},{5,13},{6,14},{7,15},{8,16},{9,17... | collective-permute-start | bytes 393224 | tf_op jit(solution)/shard_map/ppermute | solution.py:247
  21.5 7.0 %shard_map.37 = (bf16[1280,256]{1,0:T(8,128)(2,1)}, f32[2,1024,128]{2,1,0:T(8,128)}, f32[2,1024,128]{2,1,0:T(8,128)}) custom-call(bf16[1280,256]{1,0:T(8,128)(2,1)} %bitcast.13, bf16[1280,128]{1,0:T(8,128)(2,1)} %bitcast.11, bf16[1280,128]{1,0:T(8,128)(2,1)} %bitcast.12), custom_call_target="tpu_custom_call" | custom-call | flops 1677721600 | bytes 3407872 | tf_op jit(solution)/shard_map/pallas_call | solution.py:137
  28.5 4.8 %collective-permute-done.key_ref = bf16[1024,128]{1,0:T(8,128)(2,1)S(1)} collective-permute-done((bf16[1024,128]{1,0:T(8,128)(2,1)S(1)}, bf16[1024,128]{1,0:T(8,128)(2,1)S(1)}, u32[]{:S(2)}, u32[]{:S(2)}) %collective-permute-start) | collective-permute-done | bytes 262176 | tf_op jit(solution)/shard_map/ppermute | solution.py:245
  33.4 0.0 copy-start.2
  33.4 0.7 %copy-done.2 = bf16[1024,128]{1,0:T(8,128)(2,1)} copy-done((bf16[1024,128]{1,0:T(8,128)(2,1)}, bf16[1024,128]{1,0:T(8,128)(2,1)S(1)}, u32[]{:S(2)}) %copy-start.2) | copy-done | bytes 262168
  34.1 7.8 %shard_map.38 = (bf16[2,256,2560]{2,1,0:T(8,128)(2,1)}, f32[2,1024,128]{2,1,0:T(8,128)}) custom-call(s32[1]{0:T(128)} %bitcast.opening_ref, bf16[1280,256]{1,0:T(8,128)(2,1)} %bitcast.14, bf16[1024,128]{1,0:T(8,128)(2,1)} %copy-done.2, f32[2,1024,128]{2,1,0:T(8,128)} %get-tuple-element.10.stats_ref), custom_call_target="tpu_custom_call" | custom-call | flops 335544320 | bytes 5373952 | tf_op jit(solution)/shard_map/pallas_call | solution.py:169
  41.9 0.0 collective-permute-done.1.low_ref
  41.9 0.0 copy-start
  41.9 2.3 %collective-permute-done.2.high_ref = bf16[512,128]{1,0:T(8,128)(2,1)S(1)} collective-permute-done((bf16[512,128]{1,0:T(8,128)(2,1)S(1)}, bf16[512,128]{1,0:T(8,128)(2,1)S(1)}, u32[]{:S(2)}, u32[]{:S(2)}) %collective-permute-start.2) | collective-permute-done | bytes 131104 | tf_op jit(solution)/shard_map/ppermute | solution.py:247
  44.2 0.0 copy-start.1
  44.2 0.0 copy-done
  44.2 0.6 %copy-done.1 = bf16[512,128]{1,0:T(8,128)(2,1)} copy-done((bf16[512,128]{1,0:T(8,128)(2,1)}, bf16[512,128]{1,0:T(8,128)(2,1)S(1)}, u32[]{:S(2)}) %copy-start.1) | copy-done | bytes 131096
  44.8 3.6 %shard_map.39 = bf16[1280,256]{1,0:T(8,128)(2,1)} custom-call(bf16[2,256,2560]{2,1,0:T(8,128)(2,1)} %get-tuple-element.11.weight_ref, bf16[512,128]{1,0:T(8,128)(2,1)} %copy-done, bf16[512,128]{1,0:T(8,128)(2,1)} %copy-done.1, f32[2,1024,128]{2,1,0:T(8,128)} %get-tuple-element.12.merged_ref, ...), custom_call_target="tpu_custom_call", output_to_operand_aliasing={{}: (5, {})} | custom-call | flops 335544320 | bytes 6029312 | tf_op jit(solution)/shard_map/pallas_call | solution.py:202
Async XLA Ops:
  1.0 32.4 %collective-permute-start = (bf16[1024,128]{1,0:T(8,128)(2,1)S(1)}, bf16[1024,128]{1,0:T(8,128)(2,1)S(1)}, u32[]{:S(2)}, u32[]{:S(2)}) collective-permute-start(bf16[1024,128]{1,0:T(8,128)(2,1)S(1)} %slice_bitcast_fusion), channel_id=1, source_target_pairs={{0,8},{1,9},{2,10},{3,11},{4,12},{5,13},{6,14},{7,15},{8,16},{9,17... | collective-permute-start | bytes 786440 | tf_op jit(solution)/shard_map/ppermute | solution.py:245
  8.1 33.8 %collective-permute-start.1 = (bf16[512,128]{1,0:T(8,128)(2,1)S(1)}, bf16[512,128]{1,0:T(8,128)(2,1)S(1)}, u32[]{:S(2)}, u32[]{:S(2)}) collective-permute-start(bf16[512,128]{1,0:T(8,128)(2,1)S(1)} %get-tuple-element.16), channel_id=1, source_target_pairs={{0,8},{1,9},{2,10},{3,11},{4,12},{5,13},{6,14},{7,15},{8,16},{9,17... | collective-permute-start | bytes 393224 | tf_op jit(solution)/shard_map/ppermute | solution.py:248
  15.4 28.8 %collective-permute-start.2 = (bf16[512,128]{1,0:T(8,128)(2,1)S(1)}, bf16[512,128]{1,0:T(8,128)(2,1)S(1)}, u32[]{:S(2)}, u32[]{:S(2)}) collective-permute-start(bf16[512,128]{1,0:T(8,128)(2,1)S(1)} %get-tuple-element.15), channel_id=1, source_target_pairs={{0,8},{1,9},{2,10},{3,11},{4,12},{5,13},{6,14},{7,15},{8,16},{9,17... | collective-permute-start | bytes 393224 | tf_op jit(solution)/shard_map/ppermute | solution.py:247
  33.4 0.7 %copy-start.2 = (bf16[1024,128]{1,0:T(8,128)(2,1)}, bf16[1024,128]{1,0:T(8,128)(2,1)S(1)}, u32[]{:S(2)}) copy-start(bf16[1024,128]{1,0:T(8,128)(2,1)S(1)} %collective-permute-done.key_ref) | copy-start | bytes 786436
  41.9 2.3 %copy-start = (bf16[512,128]{1,0:T(8,128)(2,1)}, bf16[512,128]{1,0:T(8,128)(2,1)S(1)}, u32[]{:S(2)}) copy-start(bf16[512,128]{1,0:T(8,128)(2,1)S(1)} %collective-permute-done.1.low_ref) | copy-start | bytes 393220
  44.2 0.6 %copy-start.1 = (bf16[512,128]{1,0:T(8,128)(2,1)}, bf16[512,128]{1,0:T(8,128)(2,1)S(1)}, u32[]{:S(2)}) copy-start(bf16[512,128]{1,0:T(8,128)(2,1)S(1)} %collective-permute-done.2.high_ref) | copy-start | bytes 393220
